TPU v7x, 512 devices: a whole 4x4x16 slice. The times are simulated.
512 devices in a mesh: section: 8 (over y, core), expert: 64 (over z, x).
Axes of the slice: x: 4, y: 4, z: 16, core: 2. Of those that a mesh axis runs over, the one named last changes fastest.
Arguments:
- tokens: bfloat16 [8, 8192, 2048], P('section', 'expert'), may hold values from -6 to 6
- grad_out: bfloat16 [8, 8192, 2048], P('section', 'expert'), may hold values from -3 to 3
- expert_ids: int32 [8, 8192, 1], P('section', 'expert'), may hold values from 0 to 15; in each aligned block of 128 rows (0 to 127, 128 to 255, ..., all dimensions but the last counted through in order) at most 16 rows name the same one
- route_weight: bfloat16 [8, 8192, 1], P('section', 'expert'), may hold values from 0.25 to 1
- gate_weight: bfloat16 [8, 64, 2048, 256], P('section', 'expert'), may hold values from -0.125 to 0.125
- up_weight: bfloat16 [8, 64, 2048, 256], P('section', 'expert'), may hold values from -0.125 to 0.125
- down_weight: bfloat16 [8, 64, 256, 2048], P('section', 'expert'), may hold values from -0.1875 to 0.1875
Outputs:
- handed_grad: bfloat16 [8, 8192, 2048], P('section', 'expert')
- gate_grad: bfloat16 [8, 8192, 1], P('section', 'expert')
Inputs may be any that keep to these rules, and one draw needn't show every extreme that they name: `expert_ids`: among the route rows of one device, at most 16 name the same expert, and in every draw some expert is named by exactly 16 rows of some device.
All inputs are finite; a program needn't handle non-finite values.
Results may differ from a plain program's by a relative error of at most 0.0058.
Values may be sent and summed in bfloat16 or wider, within the bound.
No kernel may reach another device: no remote copies, remote signals or barrier semaphores. Data moves between devices by JAX's collectives and lax.ppermute only.
A program may use at most 64 MiB of HBM per device.

v0:
```python
import jax
import jax.numpy as jnp
from jax import lax
from jax.sharding import Mesh
from jax.sharding import PartitionSpec as P


SPLIT = 4
TOPK = 1
CAP = 16
PAD = 128


def from_behind(block, axis, distance):
    devices = range(lax.axis_size(axis))
    route = [((i - distance) % len(devices), i) for i in devices]
    return lax.ppermute(block, axis, route)


def ring_shift(block, axis, step):
    size = lax.axis_size(axis)
    return lax.ppermute(block, axis, [(i, (i + step) % size) for i in range(size)])


def gather_shards(weights, axis):
    left = [ring_shift(w, axis, 1) for w in weights]
    right = [ring_shift(w, axis, -1) for w in weights]
    opposite = []
    for k, (a, b) in enumerate(zip(left, right)):
        if k % 2 == 0:
            opposite.append(ring_shift(a, axis, 1))
        else:
            opposite.append(ring_shift(b, axis, -1))
    return [tuple(weights), tuple(left), tuple(right), tuple(opposite)]


def shard_terms(rows_x, rows_g, rows_p, w_gate, w_up, w_down):
    gate = jnp.dot(rows_x, w_gate, preferred_element_type=jnp.float32)
    upval = jnp.dot(rows_x, w_up, preferred_element_type=jnp.float32)
    sig = jax.nn.sigmoid(gate)
    act = gate * sig
    hidden = act * upval
    zeta = lax.dot_general(
        rows_g, w_down, (((1,), (1,)), ((), ())), preferred_element_type=jnp.float32
    )
    part_p = jnp.sum(hidden * zeta, axis=1).astype(jnp.bfloat16)
    d_hidden = rows_p.astype(jnp.float32)[:, None] * zeta
    d_gate = (d_hidden * upval * sig * (1.0 + gate * (1.0 - sig))).astype(jnp.bfloat16)
    d_up = (d_hidden * act).astype(jnp.bfloat16)
    part_x = lax.dot_general(
        d_gate, w_gate, (((1,), (1,)), ((), ())), preferred_element_type=jnp.float32
    )
    part_x = part_x + lax.dot_general(
        d_up, w_up, (((1,), (1,)), ((), ())), preferred_element_type=jnp.float32
    )
    return part_x.astype(jnp.bfloat16), part_p


def stacked_terms(rows_x, rows_g, rows_p, w_gate, w_up, w_down):
    gate = lax.dot_general(rows_x, w_gate, (((1,), (1,)), ((), ())), preferred_element_type=jnp.float32)
    upval = lax.dot_general(rows_x, w_up, (((1,), (1,)), ((), ())), preferred_element_type=jnp.float32)
    zeta = lax.dot_general(rows_g, w_down, (((1,), (2,)), ((), ())), preferred_element_type=jnp.float32)
    sig = jax.nn.sigmoid(gate)
    act = gate * sig
    hidden = act * upval
    part_p = jnp.sum(hidden * zeta, axis=2).astype(jnp.bfloat16)
    d_hidden = rows_p.astype(jnp.float32)[:, None, None] * zeta
    d_gate = (d_hidden * upval * sig * (1.0 + gate * (1.0 - sig))).astype(jnp.bfloat16)
    d_up = (d_hidden * act).astype(jnp.bfloat16)
    part_x = lax.dot_general(d_gate, w_gate, (((2,), (2,)), ((1,), (0,))), preferred_element_type=jnp.float32)
    part_x = part_x + lax.dot_general(d_up, w_up, (((2,), (2,)), ((1,), (0,))), preferred_element_type=jnp.float32)
    sum_x = jnp.sum(part_x.astype(jnp.bfloat16).astype(jnp.float32), axis=0)
    sum_p = jnp.sum(part_p.astype(jnp.float32), axis=1)
    return sum_x, sum_p


def pad_column(values, rows):
    col = jnp.zeros((rows, PAD), jnp.bfloat16)
    return col.at[:, 0].set(values.astype(jnp.bfloat16))


def device_body(tokens, grad_out, expert_ids, route_weight, gate_weight, up_weight, down_weight):
    feats = tokens[0]
    grads = grad_out[0]
    route_ids = expert_ids[0].reshape(-1)
    route_w = route_weight[0].reshape(-1)
    shards = gather_shards((gate_weight[0, 0], up_weight[0, 0], down_weight[0, 0]), "ex")
    groups = lax.axis_size("ez")
    tok_count, width = feats.shape
    rows = tok_count * TOPK
    onehot = (route_ids[:, None] == jnp.arange(groups, dtype=jnp.int32)[None, :]).astype(jnp.int32)
    before = jnp.cumsum(onehot, axis=0) - onehot
    slot = jnp.sum(before * onehot, axis=1)
    place = route_ids * CAP + slot
    table = (place[None, :] == jnp.arange(groups * CAP, dtype=jnp.int32)[:, None]).astype(
        jnp.bfloat16
    )
    packed = jnp.concatenate(
        [jnp.repeat(feats, TOPK, axis=0), jnp.repeat(grads, TOPK, axis=0), pad_column(route_w, rows)],
        axis=1,
    )
    send = jnp.dot(table, packed, preferred_element_type=jnp.float32).astype(jnp.bfloat16)
    recv = lax.all_to_all(
        send.reshape(groups, CAP, -1), "ez", split_axis=0, concat_axis=0, tiled=True
    ).reshape(groups * CAP, -1)
    rows_x = recv[:, :width]
    rows_g = recv[:, width : 2 * width]
    rows_p = recv[:, 2 * width]
    near, far = shards[:-1], shards[-1]
    w_gate = jnp.stack([w[0] for w in near])
    w_up = jnp.stack([w[1] for w in near])
    w_down = jnp.stack([w[2] for w in near])
    sum_x, sum_p = stacked_terms(rows_x, rows_g, rows_p, w_gate, w_up, w_down)
    part_x, part_p = shard_terms(rows_x, rows_g, rows_p, *far)
    sum_x = (sum_x + part_x.astype(jnp.float32)).astype(jnp.bfloat16)
    sum_p = (sum_p + part_p.astype(jnp.float32)).astype(jnp.bfloat16)
    reply = jnp.concatenate([sum_x, pad_column(sum_p, groups * CAP)], axis=1)
    back = lax.all_to_all(
        reply.reshape(groups, CAP, -1), "ez", split_axis=0, concat_axis=0, tiled=True
    ).reshape(groups * CAP, -1)
    picked = jnp.take(back, place, axis=0)
    input_grad = jnp.sum(
        picked[:, :width].astype(jnp.float32).reshape(tok_count, TOPK, width), axis=1
    ).astype(jnp.bfloat16)
    gate_grad = picked[:, width].reshape(tok_count, TOPK)
    handed = from_behind(input_grad, "section", -1)
    return (handed[None], gate_grad[None])


def solution(mesh):
    sections = mesh.shape["section"]
    experts = mesh.shape["expert"]
    grid = mesh.devices.reshape(sections, experts // SPLIT, SPLIT)
    split_mesh = Mesh(grid, ("section", "ez", "ex"))
    spec3 = P("section", ("ez", "ex"), None)
    spec4 = P("section", ("ez", "ex"), None, None)
    in_specs = (spec3, spec3, spec3, spec3, spec4, spec4, spec4)
    out_specs = (spec3, spec3)
    return jax.shard_map(device_body, mesh=split_mesh, in_specs=in_specs, out_specs=out_specs, check_vma=False)
```

profile of v0, /device:TPU:1, one launch (start us, length us, event | category | flops | bytes accessed | tf_op | source)
XLA Modules:
  0.0 233.8 jit_solution(3186940192933933743)
XLA Ops:
  0.6 0.6 compare_reduce_fusion
  1.3 1.3 fusion.49
  2.6 0.1 copy.42
  2.7 0.7 fusion.47
  3.5 0.2 reduce_window_sum.11
  3.6 0.8 select_reduce_fusion
  4.5 0.7 compare_and_fusion
  5.1 3.3 %convolution_convert_fusion = bf16[256,4224]{1,0:T(8,128)(2,1)} fusion(bf16[128,1]{1,0:T(8,128)(2,1)S(1)} %copy.42, bf16[128,2048]{1,0:T(8,128)(2,1)} %bitcast.72, bf16[128,2048]{1,0:T(8,128)(2,1)} %bitcast.73, s32[128]{0:T(128)S(1)} %get-tuple-element.27), kind=kOutput, calls=%fused_computation.1 | convolution fusion | flops 282263552 | bytes 3212032 | tf_op jit(solution)/shard_map/dot_general | solution.py:102
  8.4 0.0 copy-start
  8.4 15.9 %all-to-all-start = ((bf16[16,16,4224]{2,1,0:T(8,128)(2,1)}), bf16[16,16,4224]{2,1,0:T(8,128)(2,1)S(1)}, u32[]{:S(2)}, u32[]{:S(2)}) async-start(bf16[16,16,4224]{2,1,0:T(8,128)(2,1)} %bitcast.56), calls=%async_computation | async-start | bytes 4325376 | tf_op jit(solution)/shard_map/all_to_all | solution.py:103
  24.3 0.0 copy-done
  24.3 1.4 copy.29
  25.7 4.4 %collective-permute-start.3 = (bf16[2048,256]{0,1:T(8,128)(2,1)}, bf16[2048,256]{0,1:T(8,128)(2,1)}, u32[]{:S(2)}, u32[]{:S(2)}) collective-permute-start(bf16[2048,256]{0,1:T(8,128)(2,1)} %bitcast.57), channel_id=1, source_target_pairs={{0,3},{1,0},{2,1},{3,2},{4,7},{5,4},{6,5},{7,6},{8,11},{9,8},{10,9... | collective-permute-start | bytes 3145736 | tf_op jit(solution)/shard_map/ppermute | solution.py:22
  30.1 1.9 collective-permute-start.2
  32.0 1.5 copy.31
  33.5 2.1 collective-permute-start.4
  35.6 3.1 %collective-permute-start = (bf16[256,2048]{1,0:T(8,128)(2,1)}, bf16[256,2048]{1,0:T(8,128)(2,1)}, u32[]{:S(2)}, u32[]{:S(2)}) collective-permute-start(bf16[256,2048]{1,0:T(8,128)(2,1)} %bitcast.69), channel_id=1, source_target_pairs={{0,1},{1,2},{2,3},{3,0},{4,5},{5,6},{6,7},{7,4},{8,9},{9,10},{10,1... | collective-permute-start | bytes 3145736 | tf_op jit(solution)/shard_map/ppermute | solution.py:22
  38.8 3.4 %collective-permute-start.5 = (bf16[2048,256]{0,1:T(8,128)(2,1)S(1)}, bf16[2048,256]{0,1:T(8,128)(2,1)}, u32[]{:S(2)}, u32[]{:S(2)}) collective-permute-start(bf16[2048,256]{0,1:T(8,128)(2,1)S(1)} %bitcast.62), channel_id=1, source_target_pairs={{0,3},{1,0},{2,1},{3,2},{4,7},{5,4},{6,5},{7,6},{8,11},{9,8},{10,9... | collective-permute-start | bytes 3145736 | tf_op jit(solution)/shard_map/ppermute | solution.py:22
  42.2 9.8 %collective-permute-done.3 = bf16[2048,256]{0,1:T(8,128)(2,1)} collective-permute-done((bf16[2048,256]{0,1:T(8,128)(2,1)}, bf16[2048,256]{0,1:T(8,128)(2,1)}, u32[]{:S(2)}, u32[]{:S(2)}) %collective-permute-start.3) | collective-permute-done | bytes 1048608 | tf_op jit(solution)/shard_map/ppermute | solution.py:22
  52.0 5.3 %collective-permute-start.1 = (bf16[256,2048]{1,0:T(8,128)(2,1)}, bf16[256,2048]{1,0:T(8,128)(2,1)}, u32[]{:S(2)}, u32[]{:S(2)}) collective-permute-start(bf16[256,2048]{1,0:T(8,128)(2,1)} %bitcast.70), channel_id=1, source_target_pairs={{0,3},{1,0},{2,1},{3,2},{4,7},{5,4},{6,5},{7,6},{8,11},{9,8},{10,9... | collective-permute-start | bytes 3145736 | tf_op jit(solution)/shard_map/ppermute | solution.py:22
  57.3 0.0 collective-permute-done.2
  57.3 1.9 collective-permute-start.7
  59.2 20.3 %collective-permute-done.4 = bf16[2048,256]{0,1:T(8,128)(2,1)} collective-permute-done((bf16[2048,256]{0,1:T(8,128)(2,1)S(1)}, bf16[2048,256]{0,1:T(8,128)(2,1)}, u32[]{:S(2)}, u32[]{:S(2)}) %collective-permute-start.4) | collective-permute-done | bytes 1048608 | tf_op jit(solution)/shard_map/ppermute | solution.py:22
  79.5 1.9 collective-permute-start.8
  81.4 20.6 %collective-permute-done = bf16[256,2048]{1,0:T(8,128)(2,1)} collective-permute-done((bf16[256,2048]{1,0:T(8,128)(2,1)}, bf16[256,2048]{1,0:T(8,128)(2,1)}, u32[]{:S(2)}, u32[]{:S(2)}) %collective-permute-start) | collective-permute-done | bytes 1048608 | tf_op jit(solution)/shard_map/ppermute | solution.py:22
  102.0 1.9 collective-permute-start.6
  103.9 15.2 %all-to-all-done = bf16[16,16,4224]{2,1,0:T(8,128)(2,1)S(1)} async-done(((bf16[16,16,4224]{2,1,0:T(8,128)(2,1)}), bf16[16,16,4224]{2,1,0:T(8,128)(2,1)S(1)}, u32[]{:S(2)}, u32[]{:S(2)}) %all-to-all-start) | async-done | bytes 2162720 | tf_op jit(solution)/shard_map/all_to_all | solution.py:103
  119.1 2.9 %fusion.14 = f32[256,3,256]{0,2,1:T(8,128)S(1)} fusion(bf16[1,2048,256]{1,2,0:T(8,128)(2,1)} %bitcast.15, bf16[1,2048,256]{1,2,0:T(8,128)(2,1)} %bitcast.14, bf16[1,2048,256]{1,2,0:T(8,128)(2,1)} %bitcast.59, bf16[256,4224]{1,0:T(8,128)(2,1)S(1)} %bitcast.49), kind=kOutput, calls=%fused_computation.23 | convolution fusion | flops 814743552 | bytes 4980736 | tf_op jit(solution)/shard_map/dot_general | solution.py:61
  122.0 0.0 collective-permute-done.5
  122.0 0.0 copy-start.3
  122.0 2.6 %fusion.12 = f32[256,3,256]{0,2,1:T(8,128)S(1)} fusion(bf16[1,2048,256]{1,2,0:T(8,128)(2,1)} %bitcast.19, bf16[1,2048,256]{1,2,0:T(8,128)(2,1)} %bitcast.18, bf16[1,2048,256]{1,2,0:T(8,128)(2,1)S(1)} %bitcast.63, bf16[256,4224]{1,0:T(8,128)(2,1)S(1)} %bitcast.50), kind=kOutput, calls=%fused_computation.21 | convolution fusion | flops 814743552 | bytes 4980736 | tf_op jit(solution)/shard_map/dot_general | solution.py:60
  124.7 0.0 collective-permute-done.1
  124.7 0.0 copy-done.3
  124.7 2.6 %multiply_reduce_fusion = (bf16[256,3]{0,1:T(4,128)(2,1)S(1)}, f32[256,3,256]{0,2,1:T(8,128)S(1)}) fusion(f32[256,3,256]{0,2,1:T(8,128)S(1)} %fusion.14, f32[256,3,256]{0,2,1:T(8,128)S(1)} %fusion.12, bf16[1,256,2048]{2,1,0:T(8,128)(2,1)} %bitcast.10, bf16[1,256,2048]{2,1,0:T(8,128)(2,1)} %bitcast.9, bf16[1,256,2048]{2,1,0:T(8,128)(2,1)S(1)} %bitcast.71, ...), kind=kOutput, calls=%fused_computation.37 | convolution fusion | flops 816119040 | bytes 6555136 | tf_op jit(solution)/shard_map/dot_general | solution.py:62
  127.3 0.1 convert_reduce_fusion.1
  127.5 0.0 collective-permute-done.7
  127.5 1.7 fusion.31
  129.2 0.0 collective-permute-done.8
  129.2 1.7 fusion.33
  130.9 0.0 copy-start.1
  130.9 16.0 %collective-permute-done.6 = bf16[256,2048]{1,0:T(8,128)(2,1)} collective-permute-done((bf16[256,2048]{1,0:T(8,128)(2,1)}, bf16[256,2048]{1,0:T(8,128)(2,1)}, u32[]{:S(2)}, u32[]{:S(2)}) %collective-permute-start.6) | collective-permute-done | bytes 1048608 | tf_op jit(solution)/shard_map/ppermute | solution.py:22
  146.9 1.7 multiply_reduce_fusion.1
  148.6 0.7 broadcast_select_fusion.1
  149.3 0.1 reshape.174
  149.4 0.0 copy-done.1
  149.4 2.7 %fusion.13 = f32[3,256,2048]{2,1,0:T(8,128)S(1)} fusion(bf16[1,2048,256]{1,2,0:T(8,128)(2,1)} %bitcast.15, bf16[1,2048,256]{1,2,0:T(8,128)(2,1)} %bitcast.14, bf16[1,2048,256]{1,2,0:T(8,128)(2,1)S(1)} %bitcast.60, f32[256,3,256]{0,2,1:T(8,128)S(1)} %get-tuple-element.29, f32[256]{0:T(256)S(1)} %convert_reduce_fusion.1, f32[256,3,256]{0,2,1:T(8,128)S(1)} %fusion.12), kind=kOutput, calls=%fused_computation.22 | convolution fusion | flops 809828352 | bytes 11011072 | tf_op jit(solution)/shard_map/dot_general | solution.py:71
  152.1 3.1 %convert_reduce_fusion = f32[256,2048]{1,0:T(8,128)S(1)} fusion(f32[3,256,2048]{2,1,0:T(8,128)S(1)} %fusion.13, bf16[1,2048,256]{1,2,0:T(8,128)(2,1)} %bitcast.19, bf16[1,2048,256]{1,2,0:T(8,128)(2,1)} %bitcast.18, bf16[1,2048,256]{1,2,0:T(8,128)(2,1)S(1)} %bitcast.64, f32[256,3,256]{0,2,1:T(8,128)S(1)} %fusion.12, f32[256,3,256]{0,2,1:T(8,128)S(1)} %fusion.14, ...), kind=kOutput, calls=%fused_computation.2 | convolution fusion | flops 816381952 | bytes 13894656 | tf_op jit(solution)/shard_map/dot_general | solution.py:70
  155.1 1.7 fusion.42
  156.9 1.9 fusion.9
  158.8 0.0 copy-start.2
  158.8 1.1 fusion.15
  159.9 11.2 %all-to-all-start.1 = ((bf16[16,16,2176]{2,1,0:T(8,128)(2,1)}), bf16[16,16,2176]{2,1,0:T(8,128)(2,1)S(1)}, u32[]{:S(2)}, u32[]{:S(2)}) async-start(bf16[16,16,2176]{2,1,0:T(8,128)(2,1)} %bitcast.20), calls=%async_computation.1 | async-start | bytes 2228224 | tf_op jit(solution)/shard_map/all_to_all | solution.py:118
  171.0 0.0 copy-done.2
  171.1 48.0 %all-to-all-done.1 = bf16[16,16,2176]{2,1,0:T(8,128)(2,1)S(1)} async-done(((bf16[16,16,2176]{2,1,0:T(8,128)(2,1)}), bf16[16,16,2176]{2,1,0:T(8,128)(2,1)S(1)}, u32[]{:S(2)}, u32[]{:S(2)}) %all-to-all-start.1) | async-done | bytes 1114144 | tf_op jit(solution)/shard_map/all_to_all | solution.py:118
  219.1 1.0 gather_fusion
  220.1 0.1 broadcast_select_fusion
  220.3 4.7 %collective-permute-start.9 = (bf16[128,2048]{1,0:T(8,128)(2,1)S(1)}, bf16[128,2048]{1,0:T(8,128)(2,1)S(1)}, u32[]{:S(2)}, u32[]{:S(2)}) collective-permute-start(bf16[128,2048]{1,0:T(8,128)(2,1)S(1)} %slice.53), channel_id=1, source_target_pairs={{64,0},{128,64},{192,128},{256,192},{320,256},{384,320},{448,384},... | collective-permute-start | bytes 1572872 | tf_op jit(solution)/shard_map/ppermute | solution.py:17
  224.9 0.6 slice_reduce_fusion
  225.6 7.4 %collective-permute-done.9 = bf16[128,2048]{1,0:T(8,128)(2,1)S(1)} collective-permute-done((bf16[128,2048]{1,0:T(8,128)(2,1)S(1)}, bf16[128,2048]{1,0:T(8,128)(2,1)S(1)}, u32[]{:S(2)}, u32[]{:S(2)}) %collective-permute-start.9) | collective-permute-done | bytes 524320 | tf_op jit(solution)/shard_map/ppermute | solution.py:17
  233.0 0.8 copy.44
  (4 shorter events, 0.1 us)
Async XLA Ops:
  8.4 15.9 %copy-start = (bf16[1,1,2048,256]{3,2,1,0:T(8,128)(2,1)S(1)}, bf16[1,1,2048,256]{3,2,1,0:T(8,128)(2,1)}, u32[]{:S(2)}) copy-start(bf16[1,1,2048,256]{3,2,1,0:T(8,128)(2,1)} %param.16) | copy-start | bytes 3145732
  8.4 110.7 %all-to-all-start = ((bf16[16,16,4224]{2,1,0:T(8,128)(2,1)}), bf16[16,16,4224]{2,1,0:T(8,128)(2,1)S(1)}, u32[]{:S(2)}, u32[]{:S(2)}) async-start(bf16[16,16,4224]{2,1,0:T(8,128)(2,1)} %bitcast.56), calls=%async_computation | async-start | bytes 4325376 | tf_op jit(solution)/shard_map/all_to_all | solution.py:103
  25.7 26.2 %collective-permute-start.3 = (bf16[2048,256]{0,1:T(8,128)(2,1)}, bf16[2048,256]{0,1:T(8,128)(2,1)}, u32[]{:S(2)}, u32[]{:S(2)}) collective-permute-start(bf16[2048,256]{0,1:T(8,128)(2,1)} %bitcast.57), channel_id=1, source_target_pairs={{0,3},{1,0},{2,1},{3,2},{4,7},{5,4},{6,5},{7,6},{8,11},{9,8},{10,9... | collective-permute-start | bytes 3145736 | tf_op jit(solution)/shard_map/ppermute | solution.py:22
  30.1 27.2 %collective-permute-start.2 = (bf16[2048,256]{0,1:T(8,128)(2,1)}, bf16[2048,256]{0,1:T(8,128)(2,1)}, u32[]{:S(2)}, u32[]{:S(2)}) collective-permute-start(bf16[2048,256]{0,1:T(8,128)(2,1)} %bitcast.58), channel_id=1, source_target_pairs={{0,1},{1,2},{2,3},{3,0},{4,5},{5,6},{6,7},{7,4},{8,9},{9,10},{10,1... | collective-permute-start | bytes 3145736 | tf_op jit(solution)/shard_map/ppermute | solution.py:22
  33.5 45.9 %collective-permute-start.4 = (bf16[2048,256]{0,1:T(8,128)(2,1)S(1)}, bf16[2048,256]{0,1:T(8,128)(2,1)}, u32[]{:S(2)}, u32[]{:S(2)}) collective-permute-start(bf16[2048,256]{0,1:T(8,128)(2,1)S(1)} %bitcast.61), channel_id=1, source_target_pairs={{0,1},{1,2},{2,3},{3,0},{4,5},{5,6},{6,7},{7,4},{8,9},{9,10},{10,1... | collective-permute-start | bytes 3145736 | tf_op jit(solution)/shard_map/ppermute | solution.py:22
  35.6 66.3 %collective-permute-start = (bf16[256,2048]{1,0:T(8,128)(2,1)}, bf16[256,2048]{1,0:T(8,128)(2,1)}, u32[]{:S(2)}, u32[]{:S(2)}) collective-permute-start(bf16[256,2048]{1,0:T(8,128)(2,1)} %bitcast.69), channel_id=1, source_target_pairs={{0,1},{1,2},{2,3},{3,0},{4,5},{5,6},{6,7},{7,4},{8,9},{9,10},{10,1... | collective-permute-start | bytes 3145736 | tf_op jit(solution)/shard_map/ppermute | solution.py:22
  38.8 83.2 %collective-permute-start.5 = (bf16[2048,256]{0,1:T(8,128)(2,1)S(1)}, bf16[2048,256]{0,1:T(8,128)(2,1)}, u32[]{:S(2)}, u32[]{:S(2)}) collective-permute-start(bf16[2048,256]{0,1:T(8,128)(2,1)S(1)} %bitcast.62), channel_id=1, source_target_pairs={{0,3},{1,0},{2,1},{3,2},{4,7},{5,4},{6,5},{7,6},{8,11},{9,8},{10,9... | collective-permute-start | bytes 3145736 | tf_op jit(solution)/shard_map/ppermute | solution.py:22
  52.0 72.7 %collective-permute-start.1 = (bf16[256,2048]{1,0:T(8,128)(2,1)}, bf16[256,2048]{1,0:T(8,128)(2,1)}, u32[]{:S(2)}, u32[]{:S(2)}) collective-permute-start(bf16[256,2048]{1,0:T(8,128)(2,1)} %bitcast.70), channel_id=1, source_target_pairs={{0,3},{1,0},{2,1},{3,2},{4,7},{5,4},{6,5},{7,6},{8,11},{9,8},{10,9... | collective-permute-start | bytes 3145736 | tf_op jit(solution)/shard_map/ppermute | solution.py:22
  57.3 70.2 %collective-permute-start.7 = (bf16[2048,256]{0,1:T(8,128)(2,1)}, bf16[2048,256]{0,1:T(8,128)(2,1)}, u32[]{:S(2)}, u32[]{:S(2)}) collective-permute-start(bf16[2048,256]{0,1:T(8,128)(2,1)} %collective-permute-done.3), channel_id=1, source_target_pairs={{0,3},{1,0},{2,1},{3,2},{4,7},{5,4},{6,5},{7,6},{8,11},{9,8},{10,9... | collective-permute-start | bytes 3145736 | tf_op jit(solution)/shard_map/ppermute | solution.py:22
  79.5 49.7 %collective-permute-start.8 = (bf16[2048,256]{0,1:T(8,128)(2,1)}, bf16[2048,256]{0,1:T(8,128)(2,1)}, u32[]{:S(2)}, u32[]{:S(2)}) collective-permute-start(bf16[2048,256]{0,1:T(8,128)(2,1)} %collective-permute-done.4), channel_id=1, source_target_pairs={{0,1},{1,2},{2,3},{3,0},{4,5},{5,6},{6,7},{7,4},{8,9},{9,10},{10,1... | collective-permute-start | bytes 3145736 | tf_op jit(solution)/shard_map/ppermute | solution.py:22
  102.0 44.9 %collective-permute-start.6 = (bf16[256,2048]{1,0:T(8,128)(2,1)}, bf16[256,2048]{1,0:T(8,128)(2,1)}, u32[]{:S(2)}, u32[]{:S(2)}) collective-permute-start(bf16[256,2048]{1,0:T(8,128)(2,1)} %collective-permute-done), channel_id=1, source_target_pairs={{0,1},{1,2},{2,3},{3,0},{4,5},{5,6},{6,7},{7,4},{8,9},{9,10},{10,1... | collective-permute-start | bytes 3145736 | tf_op jit(solution)/shard_map/ppermute | solution.py:22
  122.0 2.7 %copy-start.3 = (bf16[1,1,256,2048]{3,2,1,0:T(8,128)(2,1)S(1)}, bf16[1,1,256,2048]{3,2,1,0:T(8,128)(2,1)}, u32[]{:S(2)}) copy-start(bf16[1,1,256,2048]{3,2,1,0:T(8,128)(2,1)} %param.17) | copy-start | bytes 3145732
  130.9 18.5 %copy-start.1 = (bf16[1,1,2048,256]{2,3,1,0:T(8,128)(2,1)S(1)}, bf16[1,1,2048,256]{2,3,1,0:T(8,128)(2,1)}, u32[]{:S(2)}) copy-start(bf16[1,1,2048,256]{2,3,1,0:T(8,128)(2,1)} %copy.29) | copy-start | bytes 3145732
  158.8 12.3 %copy-start.2 = (s32[1,128,1]{1,2,0:T(1,128)S(1)}, s32[1,128,1]{1,2,0:T(1,128)}, u32[]{:S(2)}) copy-start(s32[1,128,1]{1,2,0:T(1,128)} %param.13) | copy-start | bytes 1540
  159.9 59.2 %all-to-all-start.1 = ((bf16[16,16,2176]{2,1,0:T(8,128)(2,1)}), bf16[16,16,2176]{2,1,0:T(8,128)(2,1)S(1)}, u32[]{:S(2)}, u32[]{:S(2)}) async-start(bf16[16,16,2176]{2,1,0:T(8,128)(2,1)} %bitcast.20), calls=%async_computation.1 | async-start | bytes 2228224 | tf_op jit(solution)/shard_map/all_to_all | solution.py:118
  220.3 12.7 %collective-permute-start.9 = (bf16[128,2048]{1,0:T(8,128)(2,1)S(1)}, bf16[128,2048]{1,0:T(8,128)(2,1)S(1)}, u32[]{:S(2)}, u32[]{:S(2)}) collective-permute-start(bf16[128,2048]{1,0:T(8,128)(2,1)S(1)} %slice.53), channel_id=1, source_target_pairs={{64,0},{128,64},{192,128},{256,192},{320,256},{384,320},{448,384},... | collective-permute-start | bytes 1572872 | tf_op jit(solution)/shard_map/ppermute | solution.py:17
where the time goes:
time: 235 us; the launch traced here: 234 us
  waiting for transfers between devices  137 us (58%)
  starting transfers between devices  57.7 us (25%)
  matrix products  25.9 us (11%)
  other arithmetic  6.35 us (3%)
  local copies, waits for them, and re-layouts  5.63 us (2%)
    ppermute x9, waiting for transfers between devices, ring_shift(): lax.ppermute(block, axis, [(i, (i + step) % size) for i in range(size)])  66.6 us
    all_to_all x1, waiting for transfers between devices, device_body(): lax.all_to_all(reply.reshape(groups, CAP, -1), 'ez', split_axis=0, concat...  48 us
    ppermute x9, starting transfers between devices, ring_shift(): lax.ppermute(block, axis, [(i, (i + step) % size) for i in range(size)])  25.9 us
    all_to_all x1, starting transfers between devices, device_body(): lax.all_to_all(send.reshape(groups, CAP, -1), 'ez', split_axis=0, concat_...  15.9 us
    all_to_all x1, waiting for transfers between devices, device_body(): lax.all_to_all(send.reshape(groups, CAP, -1), 'ez', split_axis=0, concat_...  15.2 us
    all_to_all x1, starting transfers between devices, device_body(): lax.all_to_all(reply.reshape(groups, CAP, -1), 'ez', split_axis=0, concat...  11.2 us
    ppermute x1, waiting for transfers between devices, from_behind(): return lax.ppermute(block, axis, route)  7.43 us
  transfers between devices with their start and end apart: 12, of which 7 were waited for; matrix products, arithmetic and copies ran while one was open for 7% of the time, Pallas kernels for 0%

commit v1 on v0

--- a/solution.py
+++ b/solution.py
@@ -26,11 +26,11 @@
     left = [ring_shift(w, axis, 1) for w in weights]
     right = [ring_shift(w, axis, -1) for w in weights]
     opposite = []
-    for k, (a, b) in enumerate(zip(left, right)):
-        if k % 2 == 0:
-            opposite.append(ring_shift(a, axis, 1))
-        else:
-            opposite.append(ring_shift(b, axis, -1))
+    for a, b in zip(left, right):
+        half = a.shape[0] // 2
+        first = ring_shift(a[:half], axis, 1)
+        second = ring_shift(b[half:], axis, -1)
+        opposite.append(jnp.concatenate([first, second], axis=0))
     return [tuple(weights), tuple(left), tuple(right), tuple(opposite)]
 
 

time: 235 us -> 221 us (0.940)
  waiting for transfers between devices: 137 us -> 115 us
  starting transfers between devices: 57.7 us -> 67 us
  matrix products: 25.9 us -> 21.9 us
    all_to_all x1, waiting for transfers between devices: 15.2 us -> 0.01 us  [device_body(): lax.all_to_all(send.reshape(groups, CAP, -1), 'ez', split_axis=0, concat_...]
    ppermute x9 -> x12, starting transfers between devices: 25.9 us -> 36.3 us  [ring_shift(): lax.ppermute(block, axis, [(i, (i + step) % size) for i in range(size)])]
    ppermute x9 -> x12, waiting for transfers between devices: 66.6 us -> 59.3 us  [ring_shift(): lax.ppermute(block, axis, [(i, (i + step) % size) for i in range(size)])]
    slice x0 -> x6, local copies, waits for them, and re-layouts: none -> 2.9 us  [the longest x3 1.99 us: gather_shards(): first = ring_shift(a[:half], axis, 1)]
  transfers between devices with their start and end apart: 12 -> 15, of which waited for: 7 -> 7; matrix products, arithmetic and copies ran while one was open for 7% -> 8% of each run, Pallas kernels for 0% -> 0%
where the time goes in v1:
time: 221 us; the launch traced here: 220 us
  waiting for transfers between devices  115 us (52%)
  starting transfers between devices  67 us (30%)
  matrix products  21.9 us (10%)
  other arithmetic  7.19 us (3%)
  local copies, waits for them, and re-layouts  7.09 us (3%)
    ppermute x12, waiting for transfers between devices, ring_shift(): lax.ppermute(block, axis, [(i, (i + step) % size) for i in range(size)])  59.3 us
    all_to_all x1, waiting for transfers between devices, device_body(): lax.all_to_all(reply.reshape(groups, CAP, -1), 'ez', split_axis=0, concat...  48.6 us
    ppermute x12, starting transfers between devices, ring_shift(): lax.ppermute(block, axis, [(i, (i + step) % size) for i in range(size)])  36.3 us
    all_to_all x1, starting transfers between devices, device_body(): lax.all_to_all(send.reshape(groups, CAP, -1), 'ez', split_axis=0, concat_...  15.9 us
    all_to_all x1, starting transfers between devices, device_body(): lax.all_to_all(reply.reshape(groups, CAP, -1), 'ez', split_axis=0, concat...  11.1 us
    ppermute x1, waiting for transfers between devices, from_behind(): return lax.ppermute(block, axis, route)  7.4 us
  transfers between devices with their start and end apart: 15, of which 7 were waited for; matrix products, arithmetic and copies ran while one was open for 8% of the time, Pallas kernels for 0%

profile of v1, /device:TPU:1, one launch (start us, length us, event | category | flops | bytes accessed | tf_op | source)
XLA Modules:
  0.0 219.7 jit_solution(17410006628096183895)
XLA Ops:
  0.6 0.6 compare_reduce_fusion
  1.3 1.3 fusion.52
  2.6 0.1 copy.42
  2.7 0.7 fusion.50
  3.5 0.2 reduce_window_sum.11
  3.6 0.8 select_reduce_fusion
  4.5 0.7 compare_and_fusion
  5.1 3.3 %convolution_convert_fusion = bf16[256,4224]{1,0:T(8,128)(2,1)} fusion(bf16[128,1]{1,0:T(8,128)(2,1)S(1)} %copy.42, bf16[128,2048]{1,0:T(8,128)(2,1)} %bitcast.71, bf16[128,2048]{1,0:T(8,128)(2,1)} %bitcast.72, s32[128]{0:T(128)S(1)} %get-tuple-element.27), kind=kOutput, calls=%fused_computation.1 | convolution fusion | flops 282263552 | bytes 3212032 | tf_op jit(solution)/shard_map/dot_general | solution.py:102
  8.4 15.9 %all-to-all-start = ((bf16[16,16,4224]{2,1,0:T(8,128)(2,1)}), bf16[16,16,4224]{2,1,0:T(8,128)(2,1)}, u32[]{:S(2)}, u32[]{:S(2)}) async-start(bf16[16,16,4224]{2,1,0:T(8,128)(2,1)} %bitcast.4), calls=%async_computation | async-start | bytes 4325376 | tf_op jit(solution)/shard_map/all_to_all | solution.py:103
  24.3 0.6 copy.29
  25.0 3.1 %collective-permute-start.2 = (bf16[2048,256]{0,1:T(8,128)(2,1)S(1)}, bf16[2048,256]{0,1:T(8,128)(2,1)}, u32[]{:S(2)}, u32[]{:S(2)}) collective-permute-start(bf16[2048,256]{0,1:T(8,128)(2,1)S(1)} %bitcast.48), channel_id=1, source_target_pairs={{0,1},{1,2},{2,3},{3,0},{4,5},{5,6},{6,7},{7,4},{8,9},{9,10},{10,1... | collective-permute-start | bytes 3145736 | tf_op jit(solution)/shard_map/ppermute | solution.py:22
  28.1 0.6 copy.31
  28.8 3.1 %collective-permute-start.4 = (bf16[2048,256]{0,1:T(8,128)(2,1)S(1)}, bf16[2048,256]{0,1:T(8,128)(2,1)S(1)}, u32[]{:S(2)}, u32[]{:S(2)}) collective-permute-start(bf16[2048,256]{0,1:T(8,128)(2,1)S(1)} %bitcast.52), channel_id=1, source_target_pairs={{0,1},{1,2},{2,3},{3,0},{4,5},{5,6},{6,7},{7,4},{8,9},{9,10},{10,1... | collective-permute-start | bytes 3145736 | tf_op jit(solution)/shard_map/ppermute | solution.py:22
  31.9 3.4 %collective-permute-start.3 = (bf16[2048,256]{0,1:T(8,128)(2,1)S(1)}, bf16[2048,256]{0,1:T(8,128)(2,1)S(1)}, u32[]{:S(2)}, u32[]{:S(2)}) collective-permute-start(bf16[2048,256]{0,1:T(8,128)(2,1)S(1)} %bitcast.49), channel_id=1, source_target_pairs={{0,3},{1,0},{2,1},{3,2},{4,7},{5,4},{6,5},{7,6},{8,11},{9,8},{10,9... | collective-permute-start | bytes 3145736 | tf_op jit(solution)/shard_map/ppermute | solution.py:22
  35.3 2.2 collective-permute-start.5
  37.5 3.2 %collective-permute-start.1 = (bf16[256,2048]{1,0:T(8,128)(2,1)}, bf16[256,2048]{1,0:T(8,128)(2,1)S(1)}, u32[]{:S(2)}, u32[]{:S(2)}) collective-permute-start(bf16[256,2048]{1,0:T(8,128)(2,1)} %bitcast.68), channel_id=1, source_target_pairs={{0,3},{1,0},{2,1},{3,2},{4,7},{5,4},{6,5},{7,6},{8,11},{9,8},{10,9... | collective-permute-start | bytes 3145736 | tf_op jit(solution)/shard_map/ppermute | solution.py:22
  40.6 11.3 %collective-permute-done.2 = bf16[2048,256]{0,1:T(8,128)(2,1)} collective-permute-done((bf16[2048,256]{0,1:T(8,128)(2,1)S(1)}, bf16[2048,256]{0,1:T(8,128)(2,1)}, u32[]{:S(2)}, u32[]{:S(2)}) %collective-permute-start.2) | collective-permute-done | bytes 1048608 | tf_op jit(solution)/shard_map/ppermute | solution.py:22
  52.0 1.9 collective-permute-start
  53.9 1.1 slice.79
  55.0 19.5 %collective-permute-done.4 = bf16[2048,256]{0,1:T(8,128)(2,1)S(1)} collective-permute-done((bf16[2048,256]{0,1:T(8,128)(2,1)S(1)}, bf16[2048,256]{0,1:T(8,128)(2,1)S(1)}, u32[]{:S(2)}, u32[]{:S(2)}) %collective-permute-start.4) | collective-permute-done | bytes 1048608 | tf_op jit(solution)/shard_map/ppermute | solution.py:22
  74.4 1.9 collective-permute-start.8
  76.4 0.0 collective-permute-done.3
  76.4 0.0 copy-start.6
  76.4 3.1 %collective-permute-start.10 = (bf16[1024,256]{0,1:T(8,128)(2,1)S(1)}, bf16[1024,256]{0,1:T(8,128)(2,1)S(1)}, u32[]{:S(2)}, u32[]{:S(2)}) collective-permute-start(bf16[1024,256]{0,1:T(8,128)(2,1)S(1)} %slice.81), channel_id=1, source_target_pairs={{0,1},{1,2},{2,3},{3,0},{4,5},{5,6},{6,7},{7,4},{8,9},{9,10},{10,1... | collective-permute-start | bytes 1572872 | tf_op jit(solution)/shard_map/ppermute | solution.py:22
  79.6 0.0 collective-permute-done.5
  79.6 4.5 %collective-permute-start.9 = (bf16[1024,256]{0,1:T(8,128)(2,1)S(1)}, bf16[1024,256]{0,1:T(8,128)(2,1)S(1)}, u32[]{:S(2)}, u32[]{:S(2)}) collective-permute-start(bf16[1024,256]{0,1:T(8,128)(2,1)S(1)} %slice.80), channel_id=1, source_target_pairs={{0,3},{1,0},{2,1},{3,2},{4,7},{5,4},{6,5},{7,6},{8,11},{9,8},{10,9... | collective-permute-start | bytes 1572872 | tf_op jit(solution)/shard_map/ppermute | solution.py:22
  84.2 17.7 %collective-permute-done.1 = bf16[256,2048]{1,0:T(8,128)(2,1)S(1)} collective-permute-done((bf16[256,2048]{1,0:T(8,128)(2,1)}, bf16[256,2048]{1,0:T(8,128)(2,1)S(1)}, u32[]{:S(2)}, u32[]{:S(2)}) %collective-permute-start.1) | collective-permute-done | bytes 1048608 | tf_op jit(solution)/shard_map/ppermute | solution.py:22
  101.9 4.6 %collective-permute-start.11 = (bf16[1024,256]{0,1:T(8,128)(2,1)S(1)}, bf16[1024,256]{0,1:T(8,128)(2,1)S(1)}, u32[]{:S(2)}, u32[]{:S(2)}) collective-permute-start(bf16[1024,256]{0,1:T(8,128)(2,1)S(1)} %slice.82), channel_id=1, source_target_pairs={{0,3},{1,0},{2,1},{3,2},{4,7},{5,4},{6,5},{7,6},{8,11},{9,8},{10,9... | collective-permute-start | bytes 1572872 | tf_op jit(solution)/shard_map/ppermute | solution.py:22
  106.5 0.8 slice.78
  107.4 0.0 collective-permute-done
  107.4 1.9 collective-permute-start.7
  109.3 0.9 slice.77
  110.2 0.0 collective-permute-done.8
  110.2 3.4 %collective-permute-start.6 = (bf16[128,2048]{1,0:T(8,128)(2,1)}, bf16[128,2048]{1,0:T(8,128)(2,1)}, u32[]{:S(2)}, u32[]{:S(2)}) collective-permute-start(bf16[128,2048]{1,0:T(8,128)(2,1)} %slice.77), channel_id=1, source_target_pairs={{0,1},{1,2},{2,3},{3,0},{4,5},{5,6},{6,7},{7,4},{8,9},{9,10},{10,1... | collective-permute-start | bytes 1572872 | tf_op jit(solution)/shard_map/ppermute | solution.py:22
  113.6 5.8 %collective-permute-done.10 = bf16[1024,256]{0,1:T(8,128)(2,1)S(1)} collective-permute-done((bf16[1024,256]{0,1:T(8,128)(2,1)S(1)}, bf16[1024,256]{0,1:T(8,128)(2,1)S(1)}, u32[]{:S(2)}, u32[]{:S(2)}) %collective-permute-start.10) | collective-permute-done | bytes 524320 | tf_op jit(solution)/shard_map/ppermute | solution.py:22
  119.4 0.0 collective-permute-done.9
  119.5 5.0 %collective-permute-done.11 = bf16[1024,256]{0,1:T(8,128)(2,1)S(1)} collective-permute-done((bf16[1024,256]{0,1:T(8,128)(2,1)S(1)}, bf16[1024,256]{0,1:T(8,128)(2,1)S(1)}, u32[]{:S(2)}, u32[]{:S(2)}) %collective-permute-start.11) | collective-permute-done | bytes 524320 | tf_op jit(solution)/shard_map/ppermute | solution.py:22
  124.6 0.0 all-to-all-done
  124.6 0.9 convert_reduce_fusion.1
  125.6 3.0 %fusion.14 = f32[256,3,256]{0,2,1:T(8,128)S(1)} fusion(bf16[1,2048,256]{1,2,0:T(8,128)(2,1)} %bitcast.59, bf16[1,2048,256]{1,2,0:T(8,128)(2,1)} %bitcast.14, bf16[1,2048,256]{1,2,0:T(8,128)(2,1)S(1)} %bitcast.50, bf16[256,4224]{1,0:T(8,128)(2,1)} %bitcast.5), kind=kOutput, calls=%fused_computation.23 | convolution fusion | flops 814743552 | bytes 4980736 | tf_op jit(solution)/shard_map/dot_general | solution.py:61
  128.6 0.0 copy-start.15
  128.7 2.4 %fusion.12 = f32[256,3,256]{0,2,1:T(8,128)S(1)} fusion(bf16[1,2048,256]{1,2,0:T(8,128)(2,1)S(1)} %bitcast.61, bf16[1,2048,256]{1,2,0:T(8,128)(2,1)S(1)} %bitcast.57, bf16[1,2048,256]{1,2,0:T(8,128)(2,1)S(1)} %bitcast.54, bf16[256,4224]{1,0:T(8,128)(2,1)} %bitcast.5), kind=kOutput, calls=%fused_computation.21 | convolution fusion | flops 814743552 | bytes 4980736 | tf_op jit(solution)/shard_map/dot_general | solution.py:60
  131.1 2.3 %multiply_reduce_fusion = (bf16[256,3]{0,1:T(4,128)(2,1)S(1)}, f32[256,3,256]{0,2,1:T(8,128)S(1)}) fusion(f32[256,3,256]{0,2,1:T(8,128)S(1)} %fusion.14, f32[256,3,256]{0,2,1:T(8,128)S(1)} %fusion.12, bf16[1,256,2048]{2,1,0:T(8,128)(2,1)S(1)} %bitcast.63, bf16[1,256,2048]{2,1,0:T(8,128)(2,1)S(1)} %bitcast.64, bf16[1,256,2048]{2,1,0:T(8,128)(2,1)S(1)} %bitcast.70, ...), kind=kOutput, calls=%fused_computation.40 | convolution fusion | flops 816119040 | bytes 6555136 | tf_op jit(solution)/shard_map/dot_general | solution.py:62
  133.5 1.7 fusion.34
  135.2 1.7 fusion.36
  136.9 0.0 collective-permute-done.7
  136.9 0.0 collective-permute-done.6
  136.9 2.1 multiply_reduce_fusion.1
  139.0 0.7 broadcast_select_fusion.1
  139.7 0.1 reshape.174
  139.8 2.4 %fusion.13 = f32[3,256,2048]{2,1,0:T(8,128)S(1)} fusion(bf16[1,2048,256]{1,2,0:T(8,128)(2,1)S(1)} %bitcast.60, bf16[1,2048,256]{1,2,0:T(8,128)(2,1)} %bitcast.14, bf16[1,2048,256]{1,2,0:T(8,128)(2,1)S(1)} %bitcast.51, f32[256,3,256]{0,2,1:T(8,128)S(1)} %get-tuple-element.29, f32[256]{0:T(256)S(1)} %convert_reduce_fusion.1, f32[256,3,256]{0,2,1:T(8,128)S(1)} %fusion.12), kind=kOutput, calls=%fused_computation.22 | convolution fusion | flops 809828352 | bytes 11011072 | tf_op jit(solution)/shard_map/dot_general | solution.py:71
  142.2 1.8 convert_reduce_fusion
  144.0 0.5 fusion.45
  144.6 0.6 fusion.9
  145.1 0.0 copy-start.14
  145.2 1.1 fusion.15
  146.2 11.1 %all-to-all-start.1 = ((bf16[16,16,2176]{2,1,0:T(8,128)(2,1)}), bf16[16,16,2176]{2,1,0:T(8,128)(2,1)S(1)}, u32[]{:S(2)}, u32[]{:S(2)}) async-start(bf16[16,16,2176]{2,1,0:T(8,128)(2,1)} %bitcast.20), calls=%async_computation.1 | async-start | bytes 2228224 | tf_op jit(solution)/shard_map/all_to_all | solution.py:118
  157.4 48.6 %all-to-all-done.1 = bf16[16,16,2176]{2,1,0:T(8,128)(2,1)S(1)} async-done(((bf16[16,16,2176]{2,1,0:T(8,128)(2,1)}), bf16[16,16,2176]{2,1,0:T(8,128)(2,1)S(1)}, u32[]{:S(2)}, u32[]{:S(2)}) %all-to-all-start.1) | async-done | bytes 1114144 | tf_op jit(solution)/shard_map/all_to_all | solution.py:118
  206.0 1.0 gather_fusion
  207.0 0.1 broadcast_select_fusion
  207.2 3.7 %collective-permute-start.12 = (bf16[128,2048]{1,0:T(8,128)(2,1)S(1)}, bf16[128,2048]{1,0:T(8,128)(2,1)S(1)}, u32[]{:S(2)}, u32[]{:S(2)}) collective-permute-start(bf16[128,2048]{1,0:T(8,128)(2,1)S(1)} %slice.83), channel_id=1, source_target_pairs={{64,0},{128,64},{192,128},{256,192},{320,256},{384,320},{448,384},... | collective-permute-start | bytes 1572872 | tf_op jit(solution)/shard_map/ppermute | solution.py:17
  210.9 0.6 slice_reduce_fusion
  211.5 7.4 %collective-permute-done.12 = bf16[128,2048]{1,0:T(8,128)(2,1)S(1)} collective-permute-done((bf16[128,2048]{1,0:T(8,128)(2,1)S(1)}, bf16[128,2048]{1,0:T(8,128)(2,1)S(1)}, u32[]{:S(2)}, u32[]{:S(2)}) %collective-permute-start.12) | collective-permute-done | bytes 524320 | tf_op jit(solution)/shard_map/ppermute | solution.py:17
  218.9 0.8 copy.46
  (40 shorter events, 0.4 us)
Async XLA Ops:
  8.4 15.9 %copy-start = (bf16[1,1,2048,256]{3,2,1,0:T(8,128)(2,1)S(1)}, bf16[1,1,2048,256]{3,2,1,0:T(8,128)(2,1)}, u32[]{:S(2)}) copy-start(bf16[1,1,2048,256]{3,2,1,0:T(8,128)(2,1)} %param.16) | copy-start | bytes 3145732
  8.4 19.7 %copy-start.1 = (bf16[1,1,2048,256]{3,2,1,0:T(8,128)(2,1)S(1)}, bf16[1,1,2048,256]{3,2,1,0:T(8,128)(2,1)}, u32[]{:S(2)}) copy-start(bf16[1,1,2048,256]{3,2,1,0:T(8,128)(2,1)} %param.15) | copy-start | bytes 3145732
  8.4 116.2 %all-to-all-start = ((bf16[16,16,4224]{2,1,0:T(8,128)(2,1)}), bf16[16,16,4224]{2,1,0:T(8,128)(2,1)}, u32[]{:S(2)}, u32[]{:S(2)}) async-start(bf16[16,16,4224]{2,1,0:T(8,128)(2,1)} %bitcast.4), calls=%async_computation | async-start | bytes 4325376 | tf_op jit(solution)/shard_map/all_to_all | solution.py:103
  25.0 27.0 %collective-permute-start.2 = (bf16[2048,256]{0,1:T(8,128)(2,1)S(1)}, bf16[2048,256]{0,1:T(8,128)(2,1)}, u32[]{:S(2)}, u32[]{:S(2)}) collective-permute-start(bf16[2048,256]{0,1:T(8,128)(2,1)S(1)} %bitcast.48), channel_id=1, source_target_pairs={{0,1},{1,2},{2,3},{3,0},{4,5},{5,6},{6,7},{7,4},{8,9},{9,10},{10,1... | collective-permute-start | bytes 3145736 | tf_op jit(solution)/shard_map/ppermute | solution.py:22
  28.8 78.6 %copy-start.2 = (bf16[1,1,2048,256]{2,3,1,0:T(8,128)(2,1)}, bf16[1,1,2048,256]{2,3,1,0:T(8,128)(2,1)S(1)}, u32[]{:S(2)}) copy-start(bf16[1,1,2048,256]{2,3,1,0:T(8,128)(2,1)S(1)} %copy.31) | copy-start | bytes 3145732
  28.8 45.6 %collective-permute-start.4 = (bf16[2048,256]{0,1:T(8,128)(2,1)S(1)}, bf16[2048,256]{0,1:T(8,128)(2,1)S(1)}, u32[]{:S(2)}, u32[]{:S(2)}) collective-permute-start(bf16[2048,256]{0,1:T(8,128)(2,1)S(1)} %bitcast.52), channel_id=1, source_target_pairs={{0,1},{1,2},{2,3},{3,0},{4,5},{5,6},{6,7},{7,4},{8,9},{9,10},{10,1... | collective-permute-start | bytes 3145736 | tf_op jit(solution)/shard_map/ppermute | solution.py:22
  31.9 44.5 %collective-permute-start.3 = (bf16[2048,256]{0,1:T(8,128)(2,1)S(1)}, bf16[2048,256]{0,1:T(8,128)(2,1)S(1)}, u32[]{:S(2)}, u32[]{:S(2)}) collective-permute-start(bf16[2048,256]{0,1:T(8,128)(2,1)S(1)} %bitcast.49), channel_id=1, source_target_pairs={{0,3},{1,0},{2,1},{3,2},{4,7},{5,4},{6,5},{7,6},{8,11},{9,8},{10,9... | collective-permute-start | bytes 3145736 | tf_op jit(solution)/shard_map/ppermute | solution.py:22
  35.3 44.3 %collective-permute-start.5 = (bf16[2048,256]{0,1:T(8,128)(2,1)S(1)}, bf16[2048,256]{0,1:T(8,128)(2,1)S(1)}, u32[]{:S(2)}, u32[]{:S(2)}) collective-permute-start(bf16[2048,256]{0,1:T(8,128)(2,1)S(1)} %bitcast.53), channel_id=1, source_target_pairs={{0,3},{1,0},{2,1},{3,2},{4,7},{5,4},{6,5},{7,6},{8,11},{9,8},{10,9... | collective-permute-start | bytes 3145736 | tf_op jit(solution)/shard_map/ppermute | solution.py:22
  37.5 64.5 %collective-permute-start.1 = (bf16[256,2048]{1,0:T(8,128)(2,1)}, bf16[256,2048]{1,0:T(8,128)(2,1)S(1)}, u32[]{:S(2)}, u32[]{:S(2)}) collective-permute-start(bf16[256,2048]{1,0:T(8,128)(2,1)} %bitcast.68), channel_id=1, source_target_pairs={{0,3},{1,0},{2,1},{3,2},{4,7},{5,4},{6,5},{7,6},{8,11},{9,8},{10,9... | collective-permute-start | bytes 3145736 | tf_op jit(solution)/shard_map/ppermute | solution.py:22
  52.0 55.4 %collective-permute-start = (bf16[256,2048]{1,0:T(8,128)(2,1)}, bf16[256,2048]{1,0:T(8,128)(2,1)S(1)}, u32[]{:S(2)}, u32[]{:S(2)}) collective-permute-start(bf16[256,2048]{1,0:T(8,128)(2,1)} %bitcast.69), channel_id=1, source_target_pairs={{0,1},{1,2},{2,3},{3,0},{4,5},{5,6},{6,7},{7,4},{8,9},{9,10},{10,1... | collective-permute-start | bytes 3145736 | tf_op jit(solution)/shard_map/ppermute | solution.py:22
  74.4 2.0 copy-start.4
  74.4 35.7 %collective-permute-start.8 = (bf16[1024,256]{0,1:T(8,128)(2,1)S(1)}, bf16[1024,256]{0,1:T(8,128)(2,1)S(1)}, u32[]{:S(2)}, u32[]{:S(2)}) collective-permute-start(bf16[1024,256]{0,1:T(8,128)(2,1)S(1)} %slice.79), channel_id=1, source_target_pairs={{0,1},{1,2},{2,3},{3,0},{4,5},{5,6},{6,7},{7,4},{8,9},{9,10},{10,1... | collective-permute-start | bytes 1572872 | tf_op jit(solution)/shard_map/ppermute | solution.py:22
  76.4 3.2 %copy-start.6 = (bf16[2048,256]{0,1:T(8,128)(2,1)}, bf16[2048,256]{0,1:T(8,128)(2,1)S(1)}, u32[]{:S(2)}) copy-start(bf16[2048,256]{0,1:T(8,128)(2,1)S(1)} %collective-permute-done.3) | copy-start | bytes 3145732
  76.4 42.9 %collective-permute-start.10 = (bf16[1024,256]{0,1:T(8,128)(2,1)S(1)}, bf16[1024,256]{0,1:T(8,128)(2,1)S(1)}, u32[]{:S(2)}, u32[]{:S(2)}) collective-permute-start(bf16[1024,256]{0,1:T(8,128)(2,1)S(1)} %slice.81), channel_id=1, source_target_pairs={{0,1},{1,2},{2,3},{3,0},{4,5},{5,6},{6,7},{7,4},{8,9},{9,10},{10,1... | collective-permute-start | bytes 1572872 | tf_op jit(solution)/shard_map/ppermute | solution.py:22
  79.6 4.6 %copy-start.8 = (bf16[2048,256]{0,1:T(8,128)(2,1)}, bf16[2048,256]{0,1:T(8,128)(2,1)S(1)}, u32[]{:S(2)}) copy-start(bf16[2048,256]{0,1:T(8,128)(2,1)S(1)} %collective-permute-done.5) | copy-start | bytes 3145732
  79.6 39.8 %collective-permute-start.9 = (bf16[1024,256]{0,1:T(8,128)(2,1)S(1)}, bf16[1024,256]{0,1:T(8,128)(2,1)S(1)}, u32[]{:S(2)}, u32[]{:S(2)}) collective-permute-start(bf16[1024,256]{0,1:T(8,128)(2,1)S(1)} %slice.80), channel_id=1, source_target_pairs={{0,3},{1,0},{2,1},{3,2},{4,7},{5,4},{6,5},{7,6},{8,11},{9,8},{10,9... | collective-permute-start | bytes 1572872 | tf_op jit(solution)/shard_map/ppermute | solution.py:22
  101.9 17.5 %copy-start.10 = (bf16[256,2048]{1,0:T(8,128)(2,1)}, bf16[256,2048]{1,0:T(8,128)(2,1)S(1)}, u32[]{:S(2)}) copy-start(bf16[256,2048]{1,0:T(8,128)(2,1)S(1)} %collective-permute-done.1) | copy-start | bytes 3145732
  101.9 22.6 %collective-permute-start.11 = (bf16[1024,256]{0,1:T(8,128)(2,1)S(1)}, bf16[1024,256]{0,1:T(8,128)(2,1)S(1)}, u32[]{:S(2)}, u32[]{:S(2)}) collective-permute-start(bf16[1024,256]{0,1:T(8,128)(2,1)S(1)} %slice.82), channel_id=1, source_target_pairs={{0,3},{1,0},{2,1},{3,2},{4,7},{5,4},{6,5},{7,6},{8,11},{9,8},{10,9... | collective-permute-start | bytes 1572872 | tf_op jit(solution)/shard_map/ppermute | solution.py:22
  107.4 17.2 %copy-start.12 = (bf16[256,2048]{1,0:T(8,128)(2,1)}, bf16[256,2048]{1,0:T(8,128)(2,1)S(1)}, u32[]{:S(2)}) copy-start(bf16[256,2048]{1,0:T(8,128)(2,1)S(1)} %collective-permute-done) | copy-start | bytes 3145732
  107.4 29.6 %collective-permute-start.7 = (bf16[128,2048]{1,0:T(8,128)(2,1)}, bf16[128,2048]{1,0:T(8,128)(2,1)}, u32[]{:S(2)}, u32[]{:S(2)}) collective-permute-start(bf16[128,2048]{1,0:T(8,128)(2,1)} %slice.78), channel_id=1, source_target_pairs={{0,3},{1,0},{2,1},{3,2},{4,7},{5,4},{6,5},{7,6},{8,11},{9,8},{10,9... | collective-permute-start | bytes 1572872 | tf_op jit(solution)/shard_map/ppermute | solution.py:22
  110.2 26.8 %collective-permute-start.6 = (bf16[128,2048]{1,0:T(8,128)(2,1)}, bf16[128,2048]{1,0:T(8,128)(2,1)}, u32[]{:S(2)}, u32[]{:S(2)}) collective-permute-start(bf16[128,2048]{1,0:T(8,128)(2,1)} %slice.77), channel_id=1, source_target_pairs={{0,1},{1,2},{2,3},{3,0},{4,5},{5,6},{6,7},{7,4},{8,9},{9,10},{10,1... | collective-permute-start | bytes 1572872 | tf_op jit(solution)/shard_map/ppermute | solution.py:22
  125.5 3.1 %copy-start.3 = (bf16[1,1,2048,256]{2,3,1,0:T(8,128)(2,1)S(1)}, bf16[1,1,2048,256]{2,3,1,0:T(8,128)(2,1)}, u32[]{:S(2)}) copy-start(bf16[1,1,2048,256]{2,3,1,0:T(8,128)(2,1)} %copy-done.2) | copy-start | bytes 3145732
  125.5 3.1 %copy-start.5 = (bf16[2048,256]{0,1:T(8,128)(2,1)S(1)}, bf16[2048,256]{0,1:T(8,128)(2,1)}, u32[]{:S(2)}) copy-start(bf16[2048,256]{0,1:T(8,128)(2,1)} %copy-done.4) | copy-start | bytes 3145732
  125.5 3.1 %copy-start.9 = (bf16[2048,256]{0,1:T(8,128)(2,1)S(1)}, bf16[2048,256]{0,1:T(8,128)(2,1)}, u32[]{:S(2)}) copy-start(bf16[2048,256]{0,1:T(8,128)(2,1)} %copy-done.8) | copy-start | bytes 3145732
  128.6 2.5 %copy-start.11 = (bf16[256,2048]{1,0:T(8,128)(2,1)S(1)}, bf16[256,2048]{1,0:T(8,128)(2,1)}, u32[]{:S(2)}) copy-start(bf16[256,2048]{1,0:T(8,128)(2,1)} %copy-done.10) | copy-start | bytes 3145732
  128.6 2.5 %copy-start.13 = (bf16[256,2048]{1,0:T(8,128)(2,1)S(1)}, bf16[256,2048]{1,0:T(8,128)(2,1)}, u32[]{:S(2)}) copy-start(bf16[256,2048]{1,0:T(8,128)(2,1)} %copy-done.12) | copy-start | bytes 3145732
  128.6 2.5 %copy-start.15 = (bf16[1,1,256,2048]{3,2,1,0:T(8,128)(2,1)S(1)}, bf16[1,1,256,2048]{3,2,1,0:T(8,128)(2,1)}, u32[]{:S(2)}) copy-start(bf16[1,1,256,2048]{3,2,1,0:T(8,128)(2,1)} %param.17) | copy-start | bytes 3145732
  136.9 2.9 %copy-start.7 = (bf16[2048,256]{0,1:T(8,128)(2,1)S(1)}, bf16[2048,256]{0,1:T(8,128)(2,1)}, u32[]{:S(2)}) copy-start(bf16[2048,256]{0,1:T(8,128)(2,1)} %copy-done.6) | copy-start | bytes 3145732
  145.1 12.2 %copy-start.14 = (s32[1,128,1]{1,2,0:T(1,128)S(1)}, s32[1,128,1]{1,2,0:T(1,128)}, u32[]{:S(2)}) copy-start(s32[1,128,1]{1,2,0:T(1,128)} %param.13) | copy-start | bytes 1540
  146.2 59.7 %all-to-all-start.1 = ((bf16[16,16,2176]{2,1,0:T(8,128)(2,1)}), bf16[16,16,2176]{2,1,0:T(8,128)(2,1)S(1)}, u32[]{:S(2)}, u32[]{:S(2)}) async-start(bf16[16,16,2176]{2,1,0:T(8,128)(2,1)} %bitcast.20), calls=%async_computation.1 | async-start | bytes 2228224 | tf_op jit(solution)/shard_map/all_to_all | solution.py:118
  207.2 11.7 %collective-permute-start.12 = (bf16[128,2048]{1,0:T(8,128)(2,1)S(1)}, bf16[128,2048]{1,0:T(8,128)(2,1)S(1)}, u32[]{:S(2)}, u32[]{:S(2)}) collective-permute-start(bf16[128,2048]{1,0:T(8,128)(2,1)S(1)} %slice.83), channel_id=1, source_target_pairs={{64,0},{128,64},{192,128},{256,192},{320,256},{384,320},{448,384},... | collective-permute-start | bytes 1572872 | tf_op jit(solution)/shard_map/ppermute | solution.py:17

commit v2 on v1

--- a/solution.py
+++ b/solution.py
@@ -26,17 +26,31 @@
     left = [ring_shift(w, axis, 1) for w in weights]
     right = [ring_shift(w, axis, -1) for w in weights]
     opposite = []
-    for a, b in zip(left, right):
+    for a, b, w in zip(left, right, weights):
         half = a.shape[0] // 2
         first = ring_shift(a[:half], axis, 1)
         second = ring_shift(b[half:], axis, -1)
-        opposite.append(jnp.concatenate([first, second], axis=0))
+        if w is weights[-1]:
+            opposite.append(jnp.concatenate([first, second], axis=0))
+        else:
+            opposite.append((first, second))
     return [tuple(weights), tuple(left), tuple(right), tuple(opposite)]
 
 
-def shard_terms(rows_x, rows_g, rows_p, w_gate, w_up, w_down):
-    gate = jnp.dot(rows_x, w_gate, preferred_element_type=jnp.float32)
-    upval = jnp.dot(rows_x, w_up, preferred_element_type=jnp.float32)
+def split_terms(rows_x, rows_g, rows_p, w_gate, w_up, w_down):
+    half = w_gate[0].shape[0]
+
+    def project(pair):
+        low = jnp.dot(rows_x[:, :half], pair[0], preferred_element_type=jnp.float32)
+        return low + jnp.dot(rows_x[:, half:], pair[1], preferred_element_type=jnp.float32)
+
+    def back(d_val, pair, j):
+        return lax.dot_general(
+            d_val, pair[j], (((1,), (1,)), ((), ())), preferred_element_type=jnp.float32
+        )
+
+    gate = project(w_gate)
+    upval = project(w_up)
     sig = jax.nn.sigmoid(gate)
     act = gate * sig
     hidden = act * upval
@@ -47,13 +61,8 @@
     d_hidden = rows_p.astype(jnp.float32)[:, None] * zeta
     d_gate = (d_hidden * upval * sig * (1.0 + gate * (1.0 - sig))).astype(jnp.bfloat16)
     d_up = (d_hidden * act).astype(jnp.bfloat16)
-    part_x = lax.dot_general(
-        d_gate, w_gate, (((1,), (1,)), ((), ())), preferred_element_type=jnp.float32
-    )
-    part_x = part_x + lax.dot_general(
-        d_up, w_up, (((1,), (1,)), ((), ())), preferred_element_type=jnp.float32
-    )
-    return part_x.astype(jnp.bfloat16), part_p
+    blocks = [back(d_gate, w_gate, j) + back(d_up, w_up, j) for j in range(2)]
+    return jnp.concatenate(blocks, axis=1).astype(jnp.bfloat16), part_p
 
 
 def stacked_terms(rows_x, rows_g, rows_p, w_gate, w_up, w_down):
@@ -111,7 +120,7 @@
     w_up = jnp.stack([w[1] for w in near])
     w_down = jnp.stack([w[2] for w in near])
     sum_x, sum_p = stacked_terms(rows_x, rows_g, rows_p, w_gate, w_up, w_down)
-    part_x, part_p = shard_terms(rows_x, rows_g, rows_p, *far)
+    part_x, part_p = split_terms(rows_x, rows_g, rows_p, *far)
     sum_x = (sum_x + part_x.astype(jnp.float32)).astype(jnp.bfloat16)
     sum_p = (sum_p + part_p.astype(jnp.float32)).astype(jnp.bfloat16)
     reply = jnp.concatenate([sum_x, pad_column(sum_p, groups * CAP)], axis=1)

time: 221 us -> 221 us (level)
  waiting for transfers between devices: 115 us -> 107 us
  local copies, waits for them, and re-layouts: 7.09 us -> 14.6 us
    ppermute x12, waiting for transfers between devices: 59.3 us -> 38.1 us  [ring_shift(): lax.ppermute(block, axis, [(i, (i + step) % size) for i in range(size)])]
    all_to_all x1, waiting for transfers between devices: 0.01 us -> 13.4 us  [device_body(): lax.all_to_all(send.reshape(groups, CAP, -1), 'ez', split_axis=0, concat_...]
    slice x3, local copies, waits for them, and re-layouts: 0.91 us -> 3.6 us  [gather_shards(): second = ring_shift(b[half:], axis, -1)]
    slice x3, local copies, waits for them, and re-layouts: 1.99 us -> 4.59 us  [gather_shards(): first = ring_shift(a[:half], axis, 1)]
    unnamed x38 -> x26, local copies, waits for them, and re-layouts: 2.36 us -> 4.69 us
    dot_general x5 -> x9, matrix products: 6.59 us -> 6.65 us  [the longest x4 2.32 us: back(): lax.dot_general(d_val, pair[j], (((1,), (1,)), ((), ())), preferred_eleme...]
  transfers between devices with their start and end apart: 15 -> 15, of which waited for: 7 -> 8; matrix products, arithmetic and copies ran while one was open for 8% -> 13% of each run, Pallas kernels for 0% -> 0%
where the time goes in v2:
time: 221 us; the launch traced here: 220 us
  waiting for transfers between devices  107 us (48%)
  starting transfers between devices  68 us (31%)
  matrix products  23.1 us (10%)
  local copies, waits for them, and re-layouts  14.6 us (7%)
  other arithmetic  6.63 us (3%)
    all_to_all x1, waiting for transfers between devices, device_body(): lax.all_to_all(reply.reshape(groups, CAP, -1), 'ez', split_axis=0, concat...  48 us
    ppermute x12, waiting for transfers between devices, ring_shift(): lax.ppermute(block, axis, [(i, (i + step) % size) for i in range(size)])  38.1 us
    ppermute x12, starting transfers between devices, ring_shift(): lax.ppermute(block, axis, [(i, (i + step) % size) for i in range(size)])  36 us
    all_to_all x1, starting transfers between devices, device_body(): lax.all_to_all(send.reshape(groups, CAP, -1), 'ez', split_axis=0, concat_...  15.9 us
    all_to_all x1, waiting for transfers between devices, device_body(): lax.all_to_all(send.reshape(groups, CAP, -1), 'ez', split_axis=0, concat_...  13.4 us
    all_to_all x1, starting transfers between devices, device_body(): lax.all_to_all(reply.reshape(groups, CAP, -1), 'ez', split_axis=0, concat...  11.2 us
    ppermute x1, waiting for transfers between devices, from_behind(): return lax.ppermute(block, axis, route)  7.42 us
    ppermute x1, starting transfers between devices, from_behind(): return lax.ppermute(block, axis, route)  5 us
  transfers between devices with their start and end apart: 15, of which 8 were waited for; matrix products, arithmetic and copies ran while one was open for 13% of the time, Pallas kernels for 0%

profile of v2, /device:TPU:1, one launch (start us, length us, event | category | flops | bytes accessed | tf_op | source)
XLA Modules:
  0.0 220.2 jit_solution(6904274169424011654)
XLA Ops:
  0.6 0.6 compare_reduce_fusion
  1.3 0.7 fusion.42
  2.0 0.2 reduce_window_sum.11
  2.2 0.8 select_reduce_fusion
  3.0 0.7 compare_and_fusion
  3.7 1.3 fusion.43
  5.0 0.1 copy.42
  5.1 3.3 %convolution_convert_fusion = bf16[256,4224]{1,0:T(8,128)(2,1)} fusion(bf16[128,1]{1,0:T(8,128)(2,1)S(1)} %copy.42, bf16[128,2048]{1,0:T(8,128)(2,1)} %bitcast.82, bf16[128,2048]{1,0:T(8,128)(2,1)} %bitcast.83, s32[128]{0:T(128)S(1)} %get-tuple-element.27), kind=kOutput, calls=%fused_computation.1 | convolution fusion | flops 282263552 | bytes 3212032 | tf_op jit(solution)/shard_map/dot_general | solution.py:111
  8.4 15.9 %all-to-all-start = ((bf16[16,16,4224]{2,1,0:T(8,128)(2,1)}), bf16[16,16,4224]{2,1,0:T(8,128)(2,1)S(1)}, u32[]{:S(2)}, u32[]{:S(2)}) async-start(bf16[16,16,4224]{2,1,0:T(8,128)(2,1)} %bitcast.64), calls=%async_computation | async-start | bytes 4325376 | tf_op jit(solution)/shard_map/all_to_all | solution.py:112
  24.3 1.4 copy.29
  25.7 4.4 %collective-permute-start.3 = (bf16[2048,256]{0,1:T(8,128)(2,1)}, bf16[2048,256]{0,1:T(8,128)(2,1)S(1)}, u32[]{:S(2)}, u32[]{:S(2)}) collective-permute-start(bf16[2048,256]{0,1:T(8,128)(2,1)} %bitcast.65), channel_id=1, source_target_pairs={{0,3},{1,0},{2,1},{3,2},{4,7},{5,4},{6,5},{7,6},{8,11},{9,8},{10,9... | collective-permute-start | bytes 3145736 | tf_op jit(solution)/shard_map/ppermute | solution.py:22
  30.1 1.9 collective-permute-start.2
  32.0 2.1 collective-permute-start
  34.2 4.4 %collective-permute-start.1 = (bf16[256,2048]{1,0:T(8,128)(2,1)}, bf16[256,2048]{1,0:T(8,128)(2,1)}, u32[]{:S(2)}, u32[]{:S(2)}) collective-permute-start(bf16[256,2048]{1,0:T(8,128)(2,1)} %bitcast.80), channel_id=1, source_target_pairs={{0,3},{1,0},{2,1},{3,2},{4,7},{5,4},{6,5},{7,6},{8,11},{9,8},{10,9... | collective-permute-start | bytes 3145736 | tf_op jit(solution)/shard_map/ppermute | solution.py:22
  38.6 2.3 %copy.31 = bf16[1,1,2048,256]{2,3,1,0:T(8,128)(2,1)} copy(bf16[1,1,2048,256]{3,2,1,0:T(8,128)(2,1)} %param.15) | data formatting | bytes 2097152 | tf_op args[4]
  40.8 3.3 %collective-permute-start.5 = (bf16[2048,256]{0,1:T(8,128)(2,1)}, bf16[2048,256]{0,1:T(8,128)(2,1)S(1)}, u32[]{:S(2)}, u32[]{:S(2)}) collective-permute-start(bf16[2048,256]{0,1:T(8,128)(2,1)} %bitcast.17), channel_id=1, source_target_pairs={{0,3},{1,0},{2,1},{3,2},{4,7},{5,4},{6,5},{7,6},{8,11},{9,8},{10,9... | collective-permute-start | bytes 3145736 | tf_op jit(solution)/shard_map/ppermute | solution.py:22
  44.2 7.8 %collective-permute-done.3 = bf16[2048,256]{0,1:T(8,128)(2,1)S(1)} collective-permute-done((bf16[2048,256]{0,1:T(8,128)(2,1)}, bf16[2048,256]{0,1:T(8,128)(2,1)S(1)}, u32[]{:S(2)}, u32[]{:S(2)}) %collective-permute-start.3) | collective-permute-done | bytes 1048608 | tf_op jit(solution)/shard_map/ppermute | solution.py:22
  52.0 2.8 %collective-permute-start.4 = (bf16[2048,256]{0,1:T(8,128)(2,1)}, bf16[2048,256]{0,1:T(8,128)(2,1)S(1)}, u32[]{:S(2)}, u32[]{:S(2)}) collective-permute-start(bf16[2048,256]{0,1:T(8,128)(2,1)} %bitcast.17), channel_id=1, source_target_pairs={{0,1},{1,2},{2,3},{3,0},{4,5},{5,6},{6,7},{7,4},{8,9},{9,10},{10,1... | collective-permute-start | bytes 3145736 | tf_op jit(solution)/shard_map/ppermute | solution.py:22
  54.8 0.8 slice.94
  55.7 1.4 collective-permute-done.2
  57.0 2.9 %collective-permute-start.9 = (bf16[1024,256]{0,1:T(8,128)(2,1)}, bf16[1024,256]{0,1:T(8,128)(2,1)}, u32[]{:S(2)}, u32[]{:S(2)}) collective-permute-start(bf16[1024,256]{0,1:T(8,128)(2,1)} %slice.94), channel_id=1, source_target_pairs={{0,3},{1,0},{2,1},{3,2},{4,7},{5,4},{6,5},{7,6},{8,11},{9,8},{10,9... | collective-permute-start | bytes 1572872 | tf_op jit(solution)/shard_map/ppermute | solution.py:22
  59.9 1.9 slice.92
  61.8 17.7 %collective-permute-done = bf16[256,2048]{1,0:T(8,128)(2,1)} collective-permute-done((bf16[256,2048]{1,0:T(8,128)(2,1)}, bf16[256,2048]{1,0:T(8,128)(2,1)}, u32[]{:S(2)}, u32[]{:S(2)}) %collective-permute-start) | collective-permute-done | bytes 1048608 | tf_op jit(solution)/shard_map/ppermute | solution.py:22
  79.5 1.9 collective-permute-start.8
  81.4 1.9 slice.89
  83.3 1.9 collective-permute-start.6
  85.2 1.9 slice.90
  87.1 9.8 %collective-permute-done.5 = bf16[2048,256]{0,1:T(8,128)(2,1)S(1)} collective-permute-done((bf16[2048,256]{0,1:T(8,128)(2,1)}, bf16[2048,256]{0,1:T(8,128)(2,1)S(1)}, u32[]{:S(2)}, u32[]{:S(2)}) %collective-permute-start.5) | collective-permute-done | bytes 1048608 | tf_op jit(solution)/shard_map/ppermute | solution.py:22
  96.9 5.2 %collective-permute-start.7 = (bf16[128,2048]{1,0:T(8,128)(2,1)}, bf16[128,2048]{1,0:T(8,128)(2,1)}, u32[]{:S(2)}, u32[]{:S(2)}) collective-permute-start(bf16[128,2048]{1,0:T(8,128)(2,1)} %slice.90), channel_id=1, source_target_pairs={{0,3},{1,0},{2,1},{3,2},{4,7},{5,4},{6,5},{7,6},{8,11},{9,8},{10,9... | collective-permute-start | bytes 1572872 | tf_op jit(solution)/shard_map/ppermute | solution.py:22
  102.1 0.8 slice.96
  103.0 1.9 collective-permute-start.11
  104.9 0.8 slice.95
  105.7 13.4 %all-to-all-done = bf16[16,16,4224]{2,1,0:T(8,128)(2,1)S(1)} async-done(((bf16[16,16,4224]{2,1,0:T(8,128)(2,1)}), bf16[16,16,4224]{2,1,0:T(8,128)(2,1)S(1)}, u32[]{:S(2)}, u32[]{:S(2)}) %all-to-all-start) | async-done | bytes 2162720 | tf_op jit(solution)/shard_map/all_to_all | solution.py:112
  119.1 3.0 %fusion.10 = f32[256,3,256]{0,2,1:T(8,128)S(1)} fusion(bf16[1,2048,256]{1,2,0:T(8,128)(2,1)} %bitcast.72, bf16[1,2048,256]{1,2,0:T(8,128)(2,1)} %bitcast.74, bf16[1,2048,256]{1,2,0:T(8,128)(2,1)} %bitcast.16, bf16[256,4224]{1,0:T(8,128)(2,1)S(1)} %bitcast.55), kind=kOutput, calls=%fused_computation.21 | convolution fusion | flops 814743552 | bytes 4980736 | tf_op jit(solution)/shard_map/dot_general | solution.py:69
  122.2 3.1 %collective-permute-start.10 = (bf16[1024,256]{0,1:T(8,128)(2,1)S(1)}, bf16[1024,256]{0,1:T(8,128)(2,1)S(1)}, u32[]{:S(2)}, u32[]{:S(2)}) collective-permute-start(bf16[1024,256]{0,1:T(8,128)(2,1)S(1)} %copy-done.2), channel_id=1, source_target_pairs={{0,1},{1,2},{2,3},{3,0},{4,5},{5,6},{6,7},{7,4},{8,9},{9,10},{10,1... | collective-permute-start | bytes 1572872 | tf_op jit(solution)/shard_map/ppermute | solution.py:22
  125.3 1.4 fusion.32
  126.7 0.1 convert_reduce_fusion.1
  126.8 0.0 copy-start.10
  126.8 2.3 %fusion.12 = f32[256,3,256]{0,2,1:T(8,128)S(1)} fusion(bf16[1,2048,256]{1,2,0:T(8,128)(2,1)S(1)} %bitcast.70, bf16[1,2048,256]{1,2,0:T(8,128)(2,1)} %bitcast.14, bf16[1,2048,256]{1,2,0:T(8,128)(2,1)S(1)} %bitcast.67, bf16[256,4224]{1,0:T(8,128)(2,1)S(1)} %bitcast.58), kind=kOutput, calls=%fused_computation.23 | convolution fusion | flops 814743552 | bytes 4980736 | tf_op jit(solution)/shard_map/dot_general | solution.py:70
  129.1 1.5 collective-permute-done.11
  130.6 0.3 fusion.30
  131.0 2.6 %multiply_reduce_fusion = (bf16[256,3]{0,1:T(4,128)(2,1)S(1)}, f32[256,3,256]{0,2,1:T(8,128)S(1)}) fusion(f32[256,3,256]{0,2,1:T(8,128)S(1)} %fusion.12, f32[256,3,256]{0,2,1:T(8,128)S(1)} %fusion.10, bf16[1,256,2048]{2,1,0:T(8,128)(2,1)} %bitcast.10, bf16[1,256,2048]{2,1,0:T(8,128)(2,1)} %bitcast.9, bf16[1,256,2048]{2,1,0:T(8,128)(2,1)S(1)} %bitcast.81, ...), kind=kOutput, calls=%fused_computation.41 | convolution fusion | flops 816119040 | bytes 6555136 | tf_op jit(solution)/shard_map/dot_general | solution.py:71
  133.6 0.3 convolution_add_fusion.3
  134.0 2.3 %fusion.11 = f32[3,256,2048]{2,1,0:T(8,128)S(1)} fusion(bf16[1,2048,256]{1,2,0:T(8,128)(2,1)S(1)} %bitcast.71, bf16[1,2048,256]{1,2,0:T(8,128)(2,1)} %bitcast.14, bf16[1,2048,256]{1,2,0:T(8,128)(2,1)S(1)} %bitcast.68, f32[256,3,256]{0,2,1:T(8,128)S(1)} %get-tuple-element.32, f32[256]{0:T(256)S(1)} %convert_reduce_fusion.1, f32[256,3,256]{0,2,1:T(8,128)S(1)} %fusion.10), kind=kOutput, calls=%fused_computation.22 | convolution fusion | flops 809828352 | bytes 11011072 | tf_op jit(solution)/shard_map/dot_general | solution.py:80
  136.4 1.8 fusion.21
  138.2 2.8 %convert_reduce_fusion = f32[256,2048]{1,0:T(8,128)S(1)} fusion(f32[3,256,2048]{2,1,0:T(8,128)S(1)} %fusion.11, bf16[1,2048,256]{1,2,0:T(8,128)(2,1)S(1)} %bitcast.73, bf16[1,2048,256]{1,2,0:T(8,128)(2,1)S(1)} %bitcast.75, bf16[1,2048,256]{1,2,0:T(8,128)(2,1)} %bitcast.16, f32[256,3,256]{0,2,1:T(8,128)S(1)} %fusion.10, f32[256,3,256]{0,2,1:T(8,128)S(1)} %fusion.12, ...), kind=kOutput, calls=%fused_computation.2 | convolution fusion | flops 816381952 | bytes 13894656 | tf_op jit(solution)/shard_map/dot_general | solution.py:79
  141.1 0.5 multiply_convert_fusion.5
  141.5 0.7 broadcast_select_fusion.1
  142.2 0.1 reshape.174
  142.3 0.3 fusion.56
  142.6 1.4 fusion.57
  144.0 0.3 fusion.8
  144.3 0.3 fusion.9
  144.6 0.3 add_convert_fusion.1
  144.9 0.0 copy-start.9
  144.9 1.1 fusion.13
  146.0 11.2 %all-to-all-start.1 = ((bf16[16,16,2176]{2,1,0:T(8,128)(2,1)}), bf16[16,16,2176]{2,1,0:T(8,128)(2,1)S(1)}, u32[]{:S(2)}, u32[]{:S(2)}) async-start(bf16[16,16,2176]{2,1,0:T(8,128)(2,1)} %bitcast.20), calls=%async_computation.1 | async-start | bytes 2228224 | tf_op jit(solution)/shard_map/all_to_all | solution.py:127
  157.2 48.0 %all-to-all-done.1 = bf16[16,16,2176]{2,1,0:T(8,128)(2,1)S(1)} async-done(((bf16[16,16,2176]{2,1,0:T(8,128)(2,1)}), bf16[16,16,2176]{2,1,0:T(8,128)(2,1)S(1)}, u32[]{:S(2)}, u32[]{:S(2)}) %all-to-all-start.1) | async-done | bytes 1114144 | tf_op jit(solution)/shard_map/all_to_all | solution.py:127
  205.2 1.0 gather_fusion
  206.2 0.1 broadcast_select_fusion
  206.4 5.0 %collective-permute-start.12 = (bf16[128,2048]{1,0:T(8,128)(2,1)S(1)}, bf16[128,2048]{1,0:T(8,128)(2,1)S(1)}, u32[]{:S(2)}, u32[]{:S(2)}) collective-permute-start(bf16[128,2048]{1,0:T(8,128)(2,1)S(1)} %slice.97), channel_id=1, source_target_pairs={{64,0},{128,64},{192,128},{256,192},{320,256},{384,320},{448,384},... | collective-permute-start | bytes 1572872 | tf_op jit(solution)/shard_map/ppermute | solution.py:17
  211.4 0.6 slice_reduce_fusion
  212.0 7.4 %collective-permute-done.12 = bf16[128,2048]{1,0:T(8,128)(2,1)S(1)} collective-permute-done((bf16[128,2048]{1,0:T(8,128)(2,1)S(1)}, bf16[128,2048]{1,0:T(8,128)(2,1)S(1)}, u32[]{:S(2)}, u32[]{:S(2)}) %collective-permute-start.12) | collective-permute-done | bytes 524320 | tf_op jit(solution)/shard_map/ppermute | solution.py:17
  219.4 0.8 copy.44
  (31 shorter events, 0.1 us)
Async XLA Ops:
  8.4 15.9 %copy-start = (bf16[1,1,2048,256]{3,2,1,0:T(8,128)(2,1)S(1)}, bf16[1,1,2048,256]{3,2,1,0:T(8,128)(2,1)}, u32[]{:S(2)}) copy-start(bf16[1,1,2048,256]{3,2,1,0:T(8,128)(2,1)} %param.16) | copy-start | bytes 3145732
  8.4 110.7 %all-to-all-start = ((bf16[16,16,4224]{2,1,0:T(8,128)(2,1)}), bf16[16,16,4224]{2,1,0:T(8,128)(2,1)S(1)}, u32[]{:S(2)}, u32[]{:S(2)}) async-start(bf16[16,16,4224]{2,1,0:T(8,128)(2,1)} %bitcast.64), calls=%async_computation | async-start | bytes 4325376 | tf_op jit(solution)/shard_map/all_to_all | solution.py:112
  25.7 26.2 %collective-permute-start.3 = (bf16[2048,256]{0,1:T(8,128)(2,1)}, bf16[2048,256]{0,1:T(8,128)(2,1)S(1)}, u32[]{:S(2)}, u32[]{:S(2)}) collective-permute-start(bf16[2048,256]{0,1:T(8,128)(2,1)} %bitcast.65), channel_id=1, source_target_pairs={{0,3},{1,0},{2,1},{3,2},{4,7},{5,4},{6,5},{7,6},{8,11},{9,8},{10,9... | collective-permute-start | bytes 3145736 | tf_op jit(solution)/shard_map/ppermute | solution.py:22
  30.1 26.9 %collective-permute-start.2 = (bf16[2048,256]{0,1:T(8,128)(2,1)}, bf16[2048,256]{0,1:T(8,128)(2,1)}, u32[]{:S(2)}, u32[]{:S(2)}) collective-permute-start(bf16[2048,256]{0,1:T(8,128)(2,1)} %bitcast.66), channel_id=1, source_target_pairs={{0,1},{1,2},{2,3},{3,0},{4,5},{5,6},{6,7},{7,4},{8,9},{9,10},{10,1... | collective-permute-start | bytes 3145736 | tf_op jit(solution)/shard_map/ppermute | solution.py:22
  32.0 47.4 %collective-permute-start = (bf16[256,2048]{1,0:T(8,128)(2,1)}, bf16[256,2048]{1,0:T(8,128)(2,1)}, u32[]{:S(2)}, u32[]{:S(2)}) collective-permute-start(bf16[256,2048]{1,0:T(8,128)(2,1)} %bitcast.79), channel_id=1, source_target_pairs={{0,1},{1,2},{2,3},{3,0},{4,5},{5,6},{6,7},{7,4},{8,9},{9,10},{10,1... | collective-permute-start | bytes 3145736 | tf_op jit(solution)/shard_map/ppermute | solution.py:22
  34.2 49.1 %collective-permute-start.1 = (bf16[256,2048]{1,0:T(8,128)(2,1)}, bf16[256,2048]{1,0:T(8,128)(2,1)}, u32[]{:S(2)}, u32[]{:S(2)}) collective-permute-start(bf16[256,2048]{1,0:T(8,128)(2,1)} %bitcast.80), channel_id=1, source_target_pairs={{0,3},{1,0},{2,1},{3,2},{4,7},{5,4},{6,5},{7,6},{8,11},{9,8},{10,9... | collective-permute-start | bytes 3145736 | tf_op jit(solution)/shard_map/ppermute | solution.py:22
  40.8 56.1 %collective-permute-start.5 = (bf16[2048,256]{0,1:T(8,128)(2,1)}, bf16[2048,256]{0,1:T(8,128)(2,1)S(1)}, u32[]{:S(2)}, u32[]{:S(2)}) collective-permute-start(bf16[2048,256]{0,1:T(8,128)(2,1)} %bitcast.17), channel_id=1, source_target_pairs={{0,3},{1,0},{2,1},{3,2},{4,7},{5,4},{6,5},{7,6},{8,11},{9,8},{10,9... | collective-permute-start | bytes 3145736 | tf_op jit(solution)/shard_map/ppermute | solution.py:22
  52.0 9.9 %copy-start.3 = (bf16[2048,256]{0,1:T(8,128)(2,1)}, bf16[2048,256]{0,1:T(8,128)(2,1)S(1)}, u32[]{:S(2)}) copy-start(bf16[2048,256]{0,1:T(8,128)(2,1)S(1)} %collective-permute-done.3) | copy-start | bytes 3145732
  52.0 51.0 %collective-permute-start.4 = (bf16[2048,256]{0,1:T(8,128)(2,1)}, bf16[2048,256]{0,1:T(8,128)(2,1)S(1)}, u32[]{:S(2)}, u32[]{:S(2)}) collective-permute-start(bf16[2048,256]{0,1:T(8,128)(2,1)} %bitcast.17), channel_id=1, source_target_pairs={{0,1},{1,2},{2,3},{3,0},{4,5},{5,6},{6,7},{7,4},{8,9},{9,10},{10,1... | collective-permute-start | bytes 3145736 | tf_op jit(solution)/shard_map/ppermute | solution.py:22
  57.0 65.1 %collective-permute-start.9 = (bf16[1024,256]{0,1:T(8,128)(2,1)}, bf16[1024,256]{0,1:T(8,128)(2,1)}, u32[]{:S(2)}, u32[]{:S(2)}) collective-permute-start(bf16[1024,256]{0,1:T(8,128)(2,1)} %slice.94), channel_id=1, source_target_pairs={{0,3},{1,0},{2,1},{3,2},{4,7},{5,4},{6,5},{7,6},{8,11},{9,8},{10,9... | collective-permute-start | bytes 1572872 | tf_op jit(solution)/shard_map/ppermute | solution.py:22
  79.5 54.1 %collective-permute-start.8 = (bf16[1024,256]{0,1:T(8,128)(2,1)}, bf16[1024,256]{0,1:T(8,128)(2,1)S(1)}, u32[]{:S(2)}, u32[]{:S(2)}) collective-permute-start(bf16[1024,256]{0,1:T(8,128)(2,1)} %slice.92), channel_id=1, source_target_pairs={{0,1},{1,2},{2,3},{3,0},{4,5},{5,6},{6,7},{7,4},{8,9},{9,10},{10,1... | collective-permute-start | bytes 1572872 | tf_op jit(solution)/shard_map/ppermute | solution.py:22
  83.3 53.1 %collective-permute-start.6 = (bf16[128,2048]{1,0:T(8,128)(2,1)}, bf16[128,2048]{1,0:T(8,128)(2,1)}, u32[]{:S(2)}, u32[]{:S(2)}) collective-permute-start(bf16[128,2048]{1,0:T(8,128)(2,1)} %slice.89), channel_id=1, source_target_pairs={{0,1},{1,2},{2,3},{3,0},{4,5},{5,6},{6,7},{7,4},{8,9},{9,10},{10,1... | collective-permute-start | bytes 1572872 | tf_op jit(solution)/shard_map/ppermute | solution.py:22
  96.9 8.0 %copy-start.5 = (bf16[2048,256]{0,1:T(8,128)(2,1)}, bf16[2048,256]{0,1:T(8,128)(2,1)S(1)}, u32[]{:S(2)}) copy-start(bf16[2048,256]{0,1:T(8,128)(2,1)S(1)} %collective-permute-done.5) | copy-start | bytes 3145732
  96.9 39.5 %collective-permute-start.7 = (bf16[128,2048]{1,0:T(8,128)(2,1)}, bf16[128,2048]{1,0:T(8,128)(2,1)}, u32[]{:S(2)}, u32[]{:S(2)}) collective-permute-start(bf16[128,2048]{1,0:T(8,128)(2,1)} %slice.90), channel_id=1, source_target_pairs={{0,3},{1,0},{2,1},{3,2},{4,7},{5,4},{6,5},{7,6},{8,11},{9,8},{10,9... | collective-permute-start | bytes 1572872 | tf_op jit(solution)/shard_map/ppermute | solution.py:22
  103.0 1.9 copy-start.7
  103.0 27.6 %collective-permute-start.11 = (bf16[1024,256]{0,1:T(8,128)(2,1)}, bf16[1024,256]{0,1:T(8,128)(2,1)S(1)}, u32[]{:S(2)}, u32[]{:S(2)}) collective-permute-start(bf16[1024,256]{0,1:T(8,128)(2,1)} %slice.96), channel_id=1, source_target_pairs={{0,3},{1,0},{2,1},{3,2},{4,7},{5,4},{6,5},{7,6},{8,11},{9,8},{10,9... | collective-permute-start | bytes 1572872 | tf_op jit(solution)/shard_map/ppermute | solution.py:22
  119.1 3.0 %copy-start.2 = (bf16[1024,256]{0,1:T(8,128)(2,1)S(1)}, bf16[1024,256]{0,1:T(8,128)(2,1)}, u32[]{:S(2)}) copy-start(bf16[1024,256]{0,1:T(8,128)(2,1)} %slice.95) | copy-start | bytes 1572868
  119.1 7.7 %copy-start.1 = (bf16[1,1,2048,256]{2,3,1,0:T(8,128)(2,1)S(1)}, bf16[1,1,2048,256]{2,3,1,0:T(8,128)(2,1)}, u32[]{:S(2)}) copy-start(bf16[1,1,2048,256]{2,3,1,0:T(8,128)(2,1)} %copy.29) | copy-start | bytes 3145732
  119.1 7.7 %copy-start.4 = (bf16[2048,256]{0,1:T(8,128)(2,1)S(1)}, bf16[2048,256]{0,1:T(8,128)(2,1)}, u32[]{:S(2)}) copy-start(bf16[2048,256]{0,1:T(8,128)(2,1)} %copy-done.3) | copy-start | bytes 3145732
  122.2 18.9 %collective-permute-start.10 = (bf16[1024,256]{0,1:T(8,128)(2,1)S(1)}, bf16[1024,256]{0,1:T(8,128)(2,1)S(1)}, u32[]{:S(2)}, u32[]{:S(2)}) collective-permute-start(bf16[1024,256]{0,1:T(8,128)(2,1)S(1)} %copy-done.2), channel_id=1, source_target_pairs={{0,1},{1,2},{2,3},{3,0},{4,5},{5,6},{6,7},{7,4},{8,9},{9,10},{10,1... | collective-permute-start | bytes 1572872 | tf_op jit(solution)/shard_map/ppermute | solution.py:22
  126.8 4.1 %copy-start.10 = (bf16[1,1,256,2048]{3,2,1,0:T(8,128)(2,1)S(1)}, bf16[1,1,256,2048]{3,2,1,0:T(8,128)(2,1)}, u32[]{:S(2)}) copy-start(bf16[1,1,256,2048]{3,2,1,0:T(8,128)(2,1)} %param.17) | copy-start | bytes 3145732
  136.3 1.9 copy-start.6
  136.3 1.9 copy-start.8
  144.9 12.3 %copy-start.9 = (s32[1,128,1]{1,2,0:T(1,128)S(1)}, s32[1,128,1]{1,2,0:T(1,128)}, u32[]{:S(2)}) copy-start(s32[1,128,1]{1,2,0:T(1,128)} %param.13) | copy-start | bytes 1540
  146.0 59.2 %all-to-all-start.1 = ((bf16[16,16,2176]{2,1,0:T(8,128)(2,1)}), bf16[16,16,2176]{2,1,0:T(8,128)(2,1)S(1)}, u32[]{:S(2)}, u32[]{:S(2)}) async-start(bf16[16,16,2176]{2,1,0:T(8,128)(2,1)} %bitcast.20), calls=%async_computation.1 | async-start | bytes 2228224 | tf_op jit(solution)/shard_map/all_to_all | solution.py:127
  206.4 13.1 %collective-permute-start.12 = (bf16[128,2048]{1,0:T(8,128)(2,1)S(1)}, bf16[128,2048]{1,0:T(8,128)(2,1)S(1)}, u32[]{:S(2)}, u32[]{:S(2)}) collective-permute-start(bf16[128,2048]{1,0:T(8,128)(2,1)S(1)} %slice.97), channel_id=1, source_target_pairs={{64,0},{128,64},{192,128},{256,192},{320,256},{384,320},{448,384},... | collective-permute-start | bytes 1572872 | tf_op jit(solution)/shard_map/ppermute | solution.py:17

commit v3 on v1

--- a/solution.py
+++ b/solution.py
@@ -87,7 +87,6 @@
     shards = gather_shards((gate_weight[0, 0], up_weight[0, 0], down_weight[0, 0]), "ex")
     groups = lax.axis_size("ez")
     tok_count, width = feats.shape
-    rows = tok_count * TOPK
     onehot = (route_ids[:, None] == jnp.arange(groups, dtype=jnp.int32)[None, :]).astype(jnp.int32)
     before = jnp.cumsum(onehot, axis=0) - onehot
     slot = jnp.sum(before * onehot, axis=1)
@@ -96,7 +95,7 @@
         jnp.bfloat16
     )
     packed = jnp.concatenate(
-        [jnp.repeat(feats, TOPK, axis=0), jnp.repeat(grads, TOPK, axis=0), pad_column(route_w, rows)],
+        [jnp.repeat(feats, TOPK, axis=0), jnp.repeat(grads, TOPK, axis=0)],
         axis=1,
     )
     send = jnp.dot(table, packed, preferred_element_type=jnp.float32).astype(jnp.bfloat16)
@@ -105,7 +104,7 @@
     ).reshape(groups * CAP, -1)
     rows_x = recv[:, :width]
     rows_g = recv[:, width : 2 * width]
-    rows_p = recv[:, 2 * width]
+    rows_p = jnp.ones((recv.shape[0],), jnp.float32)
     near, far = shards[:-1], shards[-1]
     w_gate = jnp.stack([w[0] for w in near])
     w_up = jnp.stack([w[1] for w in near])
@@ -120,7 +119,10 @@
     ).reshape(groups * CAP, -1)
     picked = jnp.take(back, place, axis=0)
     input_grad = jnp.sum(
-        picked[:, :width].astype(jnp.float32).reshape(tok_count, TOPK, width), axis=1
+        (route_w.astype(jnp.float32)[:, None] * picked[:, :width].astype(jnp.float32)).reshape(
+            tok_count, TOPK, width
+        ),
+        axis=1,
     ).astype(jnp.bfloat16)
     gate_grad = picked[:, width].reshape(tok_count, TOPK)
     handed = from_behind(input_grad, "section", -1)

time: 221 us -> 218 us (0.986)
  no operation moved by 1% of the time
where the time goes in v3:
time: 218 us; the launch traced here: 217 us
  waiting for transfers between devices  115 us (53%)
  starting transfers between devices  67 us (31%)
  matrix products  21.7 us (10%)
  local copies, waits for them, and re-layouts  6.89 us (3%)
  other arithmetic  5.11 us (2%)
    ppermute x12, waiting for transfers between devices, ring_shift(): lax.ppermute(block, axis, [(i, (i + step) % size) for i in range(size)])  58.7 us
    all_to_all x1, waiting for transfers between devices, device_body(): lax.all_to_all(reply.reshape(groups, CAP, -1), 'ez', split_axis=0, concat...  48.6 us
    ppermute x12, starting transfers between devices, ring_shift(): lax.ppermute(block, axis, [(i, (i + step) % size) for i in range(size)])  36.3 us
    all_to_all x1, starting transfers between devices, device_body(): lax.all_to_all(send.reshape(groups, CAP, -1), 'ez', split_axis=0, concat_...  15.9 us
    all_to_all x1, starting transfers between devices, device_body(): lax.all_to_all(reply.reshape(groups, CAP, -1), 'ez', split_axis=0, concat...  11.1 us
    ppermute x1, waiting for transfers between devices, from_behind(): return lax.ppermute(block, axis, route)  7.41 us
  transfers between devices with their start and end apart: 15, of which 7 were waited for; matrix products, arithmetic and copies ran while one was open for 8% of the time, Pallas kernels for 0%

profile of v3, /device:TPU:1, one launch (start us, length us, event | category | flops | bytes accessed | tf_op | source)
XLA Modules:
  0.0 216.7 jit_solution(17259233406633329258)
XLA Ops:
  0.6 0.7 fusion.40
  1.4 0.2 reduce_window_sum.11
  1.5 0.8 select_reduce_fusion
  2.4 0.7 compare_and_fusion
  3.1 3.3 %convolution_convert_fusion = bf16[256,4096]{1,0:T(8,128)(2,1)} fusion(bf16[128,2048]{1,0:T(8,128)(2,1)} %bitcast.58, bf16[128,2048]{1,0:T(8,128)(2,1)} %bitcast.59, s32[128]{0:T(128)S(1)} %get-tuple-element.15), kind=kOutput, calls=%fused_computation.3 | convolution fusion | flops 271613952 | bytes 3146240 | tf_op jit(solution)/shard_map/dot_general | solution.py:101
  6.3 15.9 %all-to-all-start = ((bf16[16,16,4096]{2,1,0:T(8,128)(2,1)}), bf16[16,16,4096]{2,1,0:T(8,128)(2,1)}, u32[]{:S(2)}, u32[]{:S(2)}) async-start(bf16[16,16,4096]{2,1,0:T(8,128)(2,1)} %bitcast.4), calls=%async_computation | async-start | bytes 4194304 | tf_op jit(solution)/shard_map/all_to_all | solution.py:102
  22.3 0.6 copy.26
  22.9 3.1 %collective-permute-start.2 = (bf16[2048,256]{0,1:T(8,128)(2,1)S(1)}, bf16[2048,256]{0,1:T(8,128)(2,1)}, u32[]{:S(2)}, u32[]{:S(2)}) collective-permute-start(bf16[2048,256]{0,1:T(8,128)(2,1)S(1)} %bitcast.49), channel_id=1, source_target_pairs={{0,1},{1,2},{2,3},{3,0},{4,5},{5,6},{6,7},{7,4},{8,9},{9,10},{10,1... | collective-permute-start | bytes 3145736 | tf_op jit(solution)/shard_map/ppermute | solution.py:22
  26.1 0.6 copy.28
  26.7 3.1 %collective-permute-start.4 = (bf16[2048,256]{0,1:T(8,128)(2,1)S(1)}, bf16[2048,256]{0,1:T(8,128)(2,1)S(1)}, u32[]{:S(2)}, u32[]{:S(2)}) collective-permute-start(bf16[2048,256]{0,1:T(8,128)(2,1)S(1)} %bitcast.53), channel_id=1, source_target_pairs={{0,1},{1,2},{2,3},{3,0},{4,5},{5,6},{6,7},{7,4},{8,9},{9,10},{10,1... | collective-permute-start | bytes 3145736 | tf_op jit(solution)/shard_map/ppermute | solution.py:22
  29.9 3.4 %collective-permute-start.3 = (bf16[2048,256]{0,1:T(8,128)(2,1)S(1)}, bf16[2048,256]{0,1:T(8,128)(2,1)S(1)}, u32[]{:S(2)}, u32[]{:S(2)}) collective-permute-start(bf16[2048,256]{0,1:T(8,128)(2,1)S(1)} %bitcast.50), channel_id=1, source_target_pairs={{0,3},{1,0},{2,1},{3,2},{4,7},{5,4},{6,5},{7,6},{8,11},{9,8},{10,9... | collective-permute-start | bytes 3145736 | tf_op jit(solution)/shard_map/ppermute | solution.py:22
  33.2 2.2 collective-permute-start.5
  35.4 3.2 %collective-permute-start.1 = (bf16[256,2048]{1,0:T(8,128)(2,1)}, bf16[256,2048]{1,0:T(8,128)(2,1)S(1)}, u32[]{:S(2)}, u32[]{:S(2)}) collective-permute-start(bf16[256,2048]{1,0:T(8,128)(2,1)} %bitcast.71), channel_id=1, source_target_pairs={{0,3},{1,0},{2,1},{3,2},{4,7},{5,4},{6,5},{7,6},{8,11},{9,8},{10,9... | collective-permute-start | bytes 3145736 | tf_op jit(solution)/shard_map/ppermute | solution.py:22
  38.6 11.3 %collective-permute-done.2 = bf16[2048,256]{0,1:T(8,128)(2,1)} collective-permute-done((bf16[2048,256]{0,1:T(8,128)(2,1)S(1)}, bf16[2048,256]{0,1:T(8,128)(2,1)}, u32[]{:S(2)}, u32[]{:S(2)}) %collective-permute-start.2) | collective-permute-done | bytes 1048608 | tf_op jit(solution)/shard_map/ppermute | solution.py:22
  49.9 1.9 collective-permute-start
  51.8 1.1 slice.60
  52.9 19.5 %collective-permute-done.4 = bf16[2048,256]{0,1:T(8,128)(2,1)S(1)} collective-permute-done((bf16[2048,256]{0,1:T(8,128)(2,1)S(1)}, bf16[2048,256]{0,1:T(8,128)(2,1)S(1)}, u32[]{:S(2)}, u32[]{:S(2)}) %collective-permute-start.4) | collective-permute-done | bytes 1048608 | tf_op jit(solution)/shard_map/ppermute | solution.py:22
  72.4 1.9 collective-permute-start.8
  74.4 0.0 collective-permute-done.3
  74.4 3.1 %collective-permute-start.10 = (bf16[1024,256]{0,1:T(8,128)(2,1)S(1)}, bf16[1024,256]{0,1:T(8,128)(2,1)S(1)}, u32[]{:S(2)}, u32[]{:S(2)}) collective-permute-start(bf16[1024,256]{0,1:T(8,128)(2,1)S(1)} %slice.62), channel_id=1, source_target_pairs={{0,1},{1,2},{2,3},{3,0},{4,5},{5,6},{6,7},{7,4},{8,9},{9,10},{10,1... | collective-permute-start | bytes 1572872 | tf_op jit(solution)/shard_map/ppermute | solution.py:22
  77.5 0.0 collective-permute-done.5
  77.6 0.0 copy-start.8
  77.6 4.5 %collective-permute-start.9 = (bf16[1024,256]{0,1:T(8,128)(2,1)S(1)}, bf16[1024,256]{0,1:T(8,128)(2,1)S(1)}, u32[]{:S(2)}, u32[]{:S(2)}) collective-permute-start(bf16[1024,256]{0,1:T(8,128)(2,1)S(1)} %slice.61), channel_id=1, source_target_pairs={{0,3},{1,0},{2,1},{3,2},{4,7},{5,4},{6,5},{7,6},{8,11},{9,8},{10,9... | collective-permute-start | bytes 1572872 | tf_op jit(solution)/shard_map/ppermute | solution.py:22
  82.2 17.7 %collective-permute-done.1 = bf16[256,2048]{1,0:T(8,128)(2,1)S(1)} collective-permute-done((bf16[256,2048]{1,0:T(8,128)(2,1)}, bf16[256,2048]{1,0:T(8,128)(2,1)S(1)}, u32[]{:S(2)}, u32[]{:S(2)}) %collective-permute-start.1) | collective-permute-done | bytes 1048608 | tf_op jit(solution)/shard_map/ppermute | solution.py:22
  99.9 4.6 %collective-permute-start.11 = (bf16[1024,256]{0,1:T(8,128)(2,1)S(1)}, bf16[1024,256]{0,1:T(8,128)(2,1)S(1)}, u32[]{:S(2)}, u32[]{:S(2)}) collective-permute-start(bf16[1024,256]{0,1:T(8,128)(2,1)S(1)} %slice.63), channel_id=1, source_target_pairs={{0,3},{1,0},{2,1},{3,2},{4,7},{5,4},{6,5},{7,6},{8,11},{9,8},{10,9... | collective-permute-start | bytes 1572872 | tf_op jit(solution)/shard_map/ppermute | solution.py:22
  104.5 0.6 compare_reduce_fusion
  105.1 0.8 slice.59
  106.0 0.0 collective-permute-done
  106.0 1.9 collective-permute-start.7
  107.9 0.9 slice.58
  108.7 0.0 collective-permute-done.8
  108.7 3.4 %collective-permute-start.6 = (bf16[128,2048]{1,0:T(8,128)(2,1)}, bf16[128,2048]{1,0:T(8,128)(2,1)}, u32[]{:S(2)}, u32[]{:S(2)}) collective-permute-start(bf16[128,2048]{1,0:T(8,128)(2,1)} %slice.58), channel_id=1, source_target_pairs={{0,1},{1,2},{2,3},{3,0},{4,5},{5,6},{6,7},{7,4},{8,9},{9,10},{10,1... | collective-permute-start | bytes 1572872 | tf_op jit(solution)/shard_map/ppermute | solution.py:22
  112.1 5.2 %collective-permute-done.10 = bf16[1024,256]{0,1:T(8,128)(2,1)S(1)} collective-permute-done((bf16[1024,256]{0,1:T(8,128)(2,1)S(1)}, bf16[1024,256]{0,1:T(8,128)(2,1)S(1)}, u32[]{:S(2)}, u32[]{:S(2)}) %collective-permute-start.10) | collective-permute-done | bytes 524320 | tf_op jit(solution)/shard_map/ppermute | solution.py:22
  117.4 0.0 collective-permute-done.9
  117.4 5.1 %collective-permute-done.11 = bf16[1024,256]{0,1:T(8,128)(2,1)S(1)} collective-permute-done((bf16[1024,256]{0,1:T(8,128)(2,1)S(1)}, bf16[1024,256]{0,1:T(8,128)(2,1)S(1)}, u32[]{:S(2)}, u32[]{:S(2)}) %collective-permute-start.11) | collective-permute-done | bytes 524320 | tf_op jit(solution)/shard_map/ppermute | solution.py:22
  122.5 0.0 all-to-all-done
  122.6 3.0 %fusion.13 = f32[256,3,256]{0,2,1:T(8,128)S(1)} fusion(bf16[1,2048,256]{1,2,0:T(8,128)(2,1)} %bitcast.62, bf16[1,2048,256]{1,2,0:T(8,128)(2,1)} %bitcast.14, bf16[1,2048,256]{1,2,0:T(8,128)(2,1)S(1)} %bitcast.51, bf16[256,4096]{1,0:T(8,128)(2,1)} %bitcast.5), kind=kOutput, calls=%fused_computation.21 | convolution fusion | flops 814743552 | bytes 4980736 | tf_op jit(solution)/shard_map/dot_general | solution.py:61
  125.6 0.0 copy-done.3
  125.7 0.0 copy-start.15
  125.7 2.4 %fusion.11 = f32[256,3,256]{0,2,1:T(8,128)S(1)} fusion(bf16[1,2048,256]{1,2,0:T(8,128)(2,1)S(1)} %bitcast.64, bf16[1,2048,256]{1,2,0:T(8,128)(2,1)S(1)} %bitcast.60, bf16[1,2048,256]{1,2,0:T(8,128)(2,1)S(1)} %bitcast.55, bf16[256,4096]{1,0:T(8,128)(2,1)} %bitcast.5), kind=kOutput, calls=%fused_computation.19 | convolution fusion | flops 814743552 | bytes 4980736 | tf_op jit(solution)/shard_map/dot_general | solution.py:60
  128.1 2.3 %multiply_reduce_fusion = (bf16[256,3]{0,1:T(4,128)(2,1)S(1)}, f32[256,3,256]{0,2,1:T(8,128)S(1)}) fusion(f32[256,3,256]{0,2,1:T(8,128)S(1)} %fusion.13, f32[256,3,256]{0,2,1:T(8,128)S(1)} %fusion.11, bf16[1,256,2048]{2,1,0:T(8,128)(2,1)S(1)} %bitcast.66, bf16[1,256,2048]{2,1,0:T(8,128)(2,1)S(1)} %bitcast.67, bf16[1,256,2048]{2,1,0:T(8,128)(2,1)S(1)} %bitcast.73, ...), kind=kOutput, calls=%fused_computation.36 | convolution fusion | flops 816119040 | bytes 6555136 | tf_op jit(solution)/shard_map/dot_general | solution.py:62
  130.5 1.7 fusion.29
  132.2 1.7 fusion.31
  133.9 0.0 collective-permute-done.7
  133.9 0.0 collective-permute-done.6
  133.9 2.1 multiply_reduce_fusion.1
  136.0 0.7 broadcast_select_fusion.1
  136.7 0.1 reshape.134
  136.8 2.3 %fusion.12 = f32[3,256,2048]{2,1,0:T(8,128)S(1)} fusion(bf16[1,2048,256]{1,2,0:T(8,128)(2,1)S(1)} %bitcast.63, bf16[1,2048,256]{1,2,0:T(8,128)(2,1)} %bitcast.14, bf16[1,2048,256]{1,2,0:T(8,128)(2,1)S(1)} %bitcast.52, f32[256,3,256]{0,2,1:T(8,128)S(1)} %get-tuple-element.17, f32[256,3,256]{0,2,1:T(8,128)S(1)} %fusion.11), kind=kOutput, calls=%fused_computation.20 | convolution fusion | flops 809631744 | bytes 11010048 | tf_op jit(solution)/shard_map/dot_general | solution.py:71
  139.1 1.8 convert_reduce_fusion
  140.9 0.5 fusion.37
  141.4 0.5 fusion.9
  142.0 0.0 copy-start.14
  142.0 0.0 copy-start.16
  142.0 1.1 fusion.14
  143.1 11.1 %all-to-all-start.1 = ((bf16[16,16,2176]{2,1,0:T(8,128)(2,1)}), bf16[16,16,2176]{2,1,0:T(8,128)(2,1)S(1)}, u32[]{:S(2)}, u32[]{:S(2)}) async-start(bf16[16,16,2176]{2,1,0:T(8,128)(2,1)} %bitcast.20), calls=%async_computation.1 | async-start | bytes 2228224 | tf_op jit(solution)/shard_map/all_to_all | solution.py:117
  154.3 48.6 %all-to-all-done.1 = bf16[16,16,2176]{2,1,0:T(8,128)(2,1)S(1)} async-done(((bf16[16,16,2176]{2,1,0:T(8,128)(2,1)}), bf16[16,16,2176]{2,1,0:T(8,128)(2,1)S(1)}, u32[]{:S(2)}, u32[]{:S(2)}) %all-to-all-start.1) | async-done | bytes 1114144 | tf_op jit(solution)/shard_map/all_to_all | solution.py:117
  202.8 1.0 gather_fusion
  203.8 0.1 broadcast_select_fusion
  204.0 0.2 multiply_convert_fusion
  204.1 3.7 %collective-permute-start.12 = (bf16[128,2048]{1,0:T(8,128)(2,1)S(1)}, bf16[128,2048]{1,0:T(8,128)(2,1)S(1)}, u32[]{:S(2)}, u32[]{:S(2)}) collective-permute-start(bf16[128,2048]{1,0:T(8,128)(2,1)S(1)} %multiply_convert_fusion), channel_id=1, source_target_pairs={{64,0},{128,64},{192,128},{256,192},{320,256},{384,320},{448,384},... | collective-permute-start | bytes 1572872 | tf_op jit(solution)/shard_map/ppermute | solution.py:17
  207.8 0.6 slice_reduce_fusion
  208.4 7.4 %collective-permute-done.12 = bf16[128,2048]{1,0:T(8,128)(2,1)S(1)} collective-permute-done((bf16[128,2048]{1,0:T(8,128)(2,1)S(1)}, bf16[128,2048]{1,0:T(8,128)(2,1)S(1)}, u32[]{:S(2)}, u32[]{:S(2)}) %collective-permute-start.12) | collective-permute-done | bytes 524320 | tf_op jit(solution)/shard_map/ppermute | solution.py:17
  215.9 0.8 copy.42
  (40 shorter events, 0.4 us)
Async XLA Ops:
  3.0 19.2 %copy-start = (bf16[1,1,2048,256]{3,2,1,0:T(8,128)(2,1)S(1)}, bf16[1,1,2048,256]{3,2,1,0:T(8,128)(2,1)}, u32[]{:S(2)}) copy-start(bf16[1,1,2048,256]{3,2,1,0:T(8,128)(2,1)} %param.14) | copy-start | bytes 3145732
  6.3 19.7 %copy-start.1 = (bf16[1,1,2048,256]{3,2,1,0:T(8,128)(2,1)S(1)}, bf16[1,1,2048,256]{3,2,1,0:T(8,128)(2,1)}, u32[]{:S(2)}) copy-start(bf16[1,1,2048,256]{3,2,1,0:T(8,128)(2,1)} %param.13) | copy-start | bytes 3145732
  6.3 116.2 %all-to-all-start = ((bf16[16,16,4096]{2,1,0:T(8,128)(2,1)}), bf16[16,16,4096]{2,1,0:T(8,128)(2,1)}, u32[]{:S(2)}, u32[]{:S(2)}) async-start(bf16[16,16,4096]{2,1,0:T(8,128)(2,1)} %bitcast.4), calls=%async_computation | async-start | bytes 4194304 | tf_op jit(solution)/shard_map/all_to_all | solution.py:102
  22.9 27.0 %collective-permute-start.2 = (bf16[2048,256]{0,1:T(8,128)(2,1)S(1)}, bf16[2048,256]{0,1:T(8,128)(2,1)}, u32[]{:S(2)}, u32[]{:S(2)}) collective-permute-start(bf16[2048,256]{0,1:T(8,128)(2,1)S(1)} %bitcast.49), channel_id=1, source_target_pairs={{0,1},{1,2},{2,3},{3,0},{4,5},{5,6},{6,7},{7,4},{8,9},{9,10},{10,1... | collective-permute-start | bytes 3145736 | tf_op jit(solution)/shard_map/ppermute | solution.py:22
  26.7 82.0 %copy-start.2 = (bf16[1,1,2048,256]{2,3,1,0:T(8,128)(2,1)}, bf16[1,1,2048,256]{2,3,1,0:T(8,128)(2,1)S(1)}, u32[]{:S(2)}) copy-start(bf16[1,1,2048,256]{2,3,1,0:T(8,128)(2,1)S(1)} %copy.28) | copy-start | bytes 3145732
  26.7 45.6 %collective-permute-start.4 = (bf16[2048,256]{0,1:T(8,128)(2,1)S(1)}, bf16[2048,256]{0,1:T(8,128)(2,1)S(1)}, u32[]{:S(2)}, u32[]{:S(2)}) collective-permute-start(bf16[2048,256]{0,1:T(8,128)(2,1)S(1)} %bitcast.53), channel_id=1, source_target_pairs={{0,1},{1,2},{2,3},{3,0},{4,5},{5,6},{6,7},{7,4},{8,9},{9,10},{10,1... | collective-permute-start | bytes 3145736 | tf_op jit(solution)/shard_map/ppermute | solution.py:22
  29.9 44.5 %collective-permute-start.3 = (bf16[2048,256]{0,1:T(8,128)(2,1)S(1)}, bf16[2048,256]{0,1:T(8,128)(2,1)S(1)}, u32[]{:S(2)}, u32[]{:S(2)}) collective-permute-start(bf16[2048,256]{0,1:T(8,128)(2,1)S(1)} %bitcast.50), channel_id=1, source_target_pairs={{0,3},{1,0},{2,1},{3,2},{4,7},{5,4},{6,5},{7,6},{8,11},{9,8},{10,9... | collective-permute-start | bytes 3145736 | tf_op jit(solution)/shard_map/ppermute | solution.py:22
  33.2 44.3 %collective-permute-start.5 = (bf16[2048,256]{0,1:T(8,128)(2,1)S(1)}, bf16[2048,256]{0,1:T(8,128)(2,1)S(1)}, u32[]{:S(2)}, u32[]{:S(2)}) collective-permute-start(bf16[2048,256]{0,1:T(8,128)(2,1)S(1)} %bitcast.54), channel_id=1, source_target_pairs={{0,3},{1,0},{2,1},{3,2},{4,7},{5,4},{6,5},{7,6},{8,11},{9,8},{10,9... | collective-permute-start | bytes 3145736 | tf_op jit(solution)/shard_map/ppermute | solution.py:22
  35.4 64.5 %collective-permute-start.1 = (bf16[256,2048]{1,0:T(8,128)(2,1)}, bf16[256,2048]{1,0:T(8,128)(2,1)S(1)}, u32[]{:S(2)}, u32[]{:S(2)}) collective-permute-start(bf16[256,2048]{1,0:T(8,128)(2,1)} %bitcast.71), channel_id=1, source_target_pairs={{0,3},{1,0},{2,1},{3,2},{4,7},{5,4},{6,5},{7,6},{8,11},{9,8},{10,9... | collective-permute-start | bytes 3145736 | tf_op jit(solution)/shard_map/ppermute | solution.py:22
  49.9 56.0 %collective-permute-start = (bf16[256,2048]{1,0:T(8,128)(2,1)}, bf16[256,2048]{1,0:T(8,128)(2,1)S(1)}, u32[]{:S(2)}, u32[]{:S(2)}) collective-permute-start(bf16[256,2048]{1,0:T(8,128)(2,1)} %bitcast.72), channel_id=1, source_target_pairs={{0,1},{1,2},{2,3},{3,0},{4,5},{5,6},{6,7},{7,4},{8,9},{9,10},{10,1... | collective-permute-start | bytes 3145736 | tf_op jit(solution)/shard_map/ppermute | solution.py:22
  72.4 2.0 copy-start.4
  72.4 36.4 %collective-permute-start.8 = (bf16[1024,256]{0,1:T(8,128)(2,1)S(1)}, bf16[1024,256]{0,1:T(8,128)(2,1)S(1)}, u32[]{:S(2)}, u32[]{:S(2)}) collective-permute-start(bf16[1024,256]{0,1:T(8,128)(2,1)S(1)} %slice.60), channel_id=1, source_target_pairs={{0,1},{1,2},{2,3},{3,0},{4,5},{5,6},{6,7},{7,4},{8,9},{9,10},{10,1... | collective-permute-start | bytes 1572872 | tf_op jit(solution)/shard_map/ppermute | solution.py:22
  74.4 3.2 %copy-start.6 = (bf16[2048,256]{0,1:T(8,128)(2,1)}, bf16[2048,256]{0,1:T(8,128)(2,1)S(1)}, u32[]{:S(2)}) copy-start(bf16[2048,256]{0,1:T(8,128)(2,1)S(1)} %collective-permute-done.3) | copy-start | bytes 3145732
  74.4 42.9 %collective-permute-start.10 = (bf16[1024,256]{0,1:T(8,128)(2,1)S(1)}, bf16[1024,256]{0,1:T(8,128)(2,1)S(1)}, u32[]{:S(2)}, u32[]{:S(2)}) collective-permute-start(bf16[1024,256]{0,1:T(8,128)(2,1)S(1)} %slice.62), channel_id=1, source_target_pairs={{0,1},{1,2},{2,3},{3,0},{4,5},{5,6},{6,7},{7,4},{8,9},{9,10},{10,1... | collective-permute-start | bytes 1572872 | tf_op jit(solution)/shard_map/ppermute | solution.py:22
  77.6 4.6 %copy-start.8 = (bf16[2048,256]{0,1:T(8,128)(2,1)}, bf16[2048,256]{0,1:T(8,128)(2,1)S(1)}, u32[]{:S(2)}) copy-start(bf16[2048,256]{0,1:T(8,128)(2,1)S(1)} %collective-permute-done.5) | copy-start | bytes 3145732
  77.6 39.8 %collective-permute-start.9 = (bf16[1024,256]{0,1:T(8,128)(2,1)S(1)}, bf16[1024,256]{0,1:T(8,128)(2,1)S(1)}, u32[]{:S(2)}, u32[]{:S(2)}) collective-permute-start(bf16[1024,256]{0,1:T(8,128)(2,1)S(1)} %slice.61), channel_id=1, source_target_pairs={{0,3},{1,0},{2,1},{3,2},{4,7},{5,4},{6,5},{7,6},{8,11},{9,8},{10,9... | collective-permute-start | bytes 1572872 | tf_op jit(solution)/shard_map/ppermute | solution.py:22
  99.9 22.6 %copy-start.10 = (bf16[256,2048]{1,0:T(8,128)(2,1)}, bf16[256,2048]{1,0:T(8,128)(2,1)S(1)}, u32[]{:S(2)}) copy-start(bf16[256,2048]{1,0:T(8,128)(2,1)S(1)} %collective-permute-done.1) | copy-start | bytes 3145732
  99.9 22.6 %collective-permute-start.11 = (bf16[1024,256]{0,1:T(8,128)(2,1)S(1)}, bf16[1024,256]{0,1:T(8,128)(2,1)S(1)}, u32[]{:S(2)}, u32[]{:S(2)}) collective-permute-start(bf16[1024,256]{0,1:T(8,128)(2,1)S(1)} %slice.63), channel_id=1, source_target_pairs={{0,3},{1,0},{2,1},{3,2},{4,7},{5,4},{6,5},{7,6},{8,11},{9,8},{10,9... | collective-permute-start | bytes 1572872 | tf_op jit(solution)/shard_map/ppermute | solution.py:22
  106.0 16.5 %copy-start.12 = (bf16[256,2048]{1,0:T(8,128)(2,1)}, bf16[256,2048]{1,0:T(8,128)(2,1)S(1)}, u32[]{:S(2)}) copy-start(bf16[256,2048]{1,0:T(8,128)(2,1)S(1)} %collective-permute-done) | copy-start | bytes 3145732
  106.0 27.9 %collective-permute-start.7 = (bf16[128,2048]{1,0:T(8,128)(2,1)}, bf16[128,2048]{1,0:T(8,128)(2,1)}, u32[]{:S(2)}, u32[]{:S(2)}) collective-permute-start(bf16[128,2048]{1,0:T(8,128)(2,1)} %slice.59), channel_id=1, source_target_pairs={{0,3},{1,0},{2,1},{3,2},{4,7},{5,4},{6,5},{7,6},{8,11},{9,8},{10,9... | collective-permute-start | bytes 1572872 | tf_op jit(solution)/shard_map/ppermute | solution.py:22
  108.7 25.2 %collective-permute-start.6 = (bf16[128,2048]{1,0:T(8,128)(2,1)}, bf16[128,2048]{1,0:T(8,128)(2,1)}, u32[]{:S(2)}, u32[]{:S(2)}) collective-permute-start(bf16[128,2048]{1,0:T(8,128)(2,1)} %slice.58), channel_id=1, source_target_pairs={{0,1},{1,2},{2,3},{3,0},{4,5},{5,6},{6,7},{7,4},{8,9},{9,10},{10,1... | collective-permute-start | bytes 1572872 | tf_op jit(solution)/shard_map/ppermute | solution.py:22
  122.5 3.1 %copy-start.3 = (bf16[1,1,2048,256]{2,3,1,0:T(8,128)(2,1)S(1)}, bf16[1,1,2048,256]{2,3,1,0:T(8,128)(2,1)}, u32[]{:S(2)}) copy-start(bf16[1,1,2048,256]{2,3,1,0:T(8,128)(2,1)} %copy-done.2) | copy-start | bytes 3145732
  122.5 3.1 %copy-start.5 = (bf16[2048,256]{0,1:T(8,128)(2,1)S(1)}, bf16[2048,256]{0,1:T(8,128)(2,1)}, u32[]{:S(2)}) copy-start(bf16[2048,256]{0,1:T(8,128)(2,1)} %copy-done.4) | copy-start | bytes 3145732
  122.6 3.1 %copy-start.9 = (bf16[2048,256]{0,1:T(8,128)(2,1)S(1)}, bf16[2048,256]{0,1:T(8,128)(2,1)}, u32[]{:S(2)}) copy-start(bf16[2048,256]{0,1:T(8,128)(2,1)} %copy-done.8) | copy-start | bytes 3145732
  125.6 2.4 %copy-start.11 = (bf16[256,2048]{1,0:T(8,128)(2,1)S(1)}, bf16[256,2048]{1,0:T(8,128)(2,1)}, u32[]{:S(2)}) copy-start(bf16[256,2048]{1,0:T(8,128)(2,1)} %copy-done.10) | copy-start | bytes 3145732
  125.6 2.4 %copy-start.13 = (bf16[256,2048]{1,0:T(8,128)(2,1)S(1)}, bf16[256,2048]{1,0:T(8,128)(2,1)}, u32[]{:S(2)}) copy-start(bf16[256,2048]{1,0:T(8,128)(2,1)} %copy-done.12) | copy-start | bytes 3145732
  125.7 2.4 %copy-start.15 = (bf16[1,1,256,2048]{3,2,1,0:T(8,128)(2,1)S(1)}, bf16[1,1,256,2048]{3,2,1,0:T(8,128)(2,1)}, u32[]{:S(2)}) copy-start(bf16[1,1,256,2048]{3,2,1,0:T(8,128)(2,1)} %param.15) | copy-start | bytes 3145732
  133.9 2.9 %copy-start.7 = (bf16[2048,256]{0,1:T(8,128)(2,1)S(1)}, bf16[2048,256]{0,1:T(8,128)(2,1)}, u32[]{:S(2)}) copy-start(bf16[2048,256]{0,1:T(8,128)(2,1)} %copy-done.6) | copy-start | bytes 3145732
  142.0 12.3 %copy-start.14 = (s32[1,128,1]{1,2,0:T(1,128)S(1)}, s32[1,128,1]{1,2,0:T(1,128)}, u32[]{:S(2)}) copy-start(s32[1,128,1]{1,2,0:T(1,128)} %param.11) | copy-start | bytes 1540
  142.0 12.3 %copy-start.16 = (bf16[1,128,1]{1,2,0:T(2,128)(2,1)S(1)}, bf16[1,128,1]{1,2,0:T(2,128)(2,1)}, u32[]{:S(2)}) copy-start(bf16[1,128,1]{1,2,0:T(2,128)(2,1)} %param.12) | copy-start | bytes 772
  143.1 59.8 %all-to-all-start.1 = ((bf16[16,16,2176]{2,1,0:T(8,128)(2,1)}), bf16[16,16,2176]{2,1,0:T(8,128)(2,1)S(1)}, u32[]{:S(2)}, u32[]{:S(2)}) async-start(bf16[16,16,2176]{2,1,0:T(8,128)(2,1)} %bitcast.20), calls=%async_computation.1 | async-start | bytes 2228224 | tf_op jit(solution)/shard_map/all_to_all | solution.py:117
  204.1 11.7 %collective-permute-start.12 = (bf16[128,2048]{1,0:T(8,128)(2,1)S(1)}, bf16[128,2048]{1,0:T(8,128)(2,1)S(1)}, u32[]{:S(2)}, u32[]{:S(2)}) collective-permute-start(bf16[128,2048]{1,0:T(8,128)(2,1)S(1)} %multiply_convert_fusion), channel_id=1, source_target_pairs={{64,0},{128,64},{192,128},{256,192},{320,256},{384,320},{448,384},... | collective-permute-start | bytes 1572872 | tf_op jit(solution)/shard_map/ppermute | solution.py:17
